TPU v7x, 256 devices: a whole 4x4x8 slice. The times are simulated.
256 devices in a mesh: row: 8 (over z_hi, x), col: 32 (over z_lo, y, core).
Axes of the slice: x: 4, y: 4, z: 8 (z_hi: 2, z_lo: 4; z = z_hi * 4 + z_lo), core: 2. Of those that a mesh axis runs over, the one named last changes fastest.
Arguments:
- region_factors: bfloat16 [262144, 512], P(('row', 'col')), may hold values from -1.25 to 1.25
- item_factors: bfloat16 [32, 128, 512], P('col', 'row'), may hold values from -1.25 to 1.25
- slab_blocks: bfloat16 [256, 32, 6, 128, 128], P(('row', 'col')), may hold values from -6 to 6
- block_rows: int32 [256, 32, 6], P(('row', 'col')), may hold values from 0 to 7, as said below
- counts: int32 [256, 32], P(('row', 'col')), may hold values from 1 to 6, as said below
Outputs:
- new_regions: float32 [262144, 512], P(('row', 'col'))
- new_items: float32 [32, 128, 512], P('col', 'row')
Inputs may be any that keep to these rules, and one draw needn't show every extreme that they name: `counts`: every entry is at least 1; some device-block has exactly 6 present blocks in some block column. `block_rows`: for each device-block and block column, the first counts[d, p] entries are distinct; entries at slots s >= counts[d, p] (and their slab blocks) are not used.
All inputs are finite; a program needn't handle non-finite values.
Results may differ from a plain program's by a relative error of at most 0.0023.
Values may be sent and summed in bfloat16 or wider, within the bound.
No kernel may reach another device: no remote copies, remote signals or barrier semaphores. Data moves between devices by JAX's collectives and lax.ppermute only.
A program may use at most 128 MiB of HBM per device.

v0:
```python
import functools

import jax
import jax.numpy as jnp
from jax import lax
from jax.experimental import pallas as pl
from jax.experimental.pallas import tpu as pltpu
from jax.sharding import Mesh
from jax.sharding import PartitionSpec as P

region_rate = 0.05
item_rate = 0.01
decay_rate = 0.1

AXES = ("zh", "x", "zl", "y", "core")
Z_RING = ("zh", "zl")


def grad_kernel(first, last, ny, rows_ref, counts_ref, sel_ref, u_ref, v_ref, slab0_ref, slab1_ref, *rest):
    if first:
        region_ref, item_ref = rest
    else:
        region_in_ref, region_ref, item_ref = rest
    step = pl.program_id(0)
    slots, block = slab0_ref.shape[1], slab0_ref.shape[2]
    pairs = ny // 2
    zl = step // pairs
    pair = step % pairs

    @pl.when(step == 0)
    def _():
        if first:
            region_ref[...] = jnp.zeros_like(region_ref)
        else:
            region_ref[...] = region_in_ref[...]

    for g, slab_ref in enumerate((slab0_ref, slab1_ref)):
        panel = (zl * ny + 2 * pair + g) * 2 + sel_ref[0]
        count = counts_ref[panel]
        v = v_ref[g, 0]
        chosen_rows = [rows_ref[panel * slots + s] for s in range(slots)]
        chosen = jnp.concatenate([u_ref[b] for b in chosen_rows], axis=0)
        predicted = lax.dot_general(
            chosen, v, (((1,), (1,)), ((), ())), preferred_element_type=jnp.float32
        )
        tiles = slab_ref[0].reshape(slots * block, block).astype(jnp.float32)
        slot_of = lax.broadcasted_iota(jnp.int32, (slots * block, block), 0) // block
        residual = jnp.where(slot_of < count, predicted - tiles, 0.0).astype(jnp.bfloat16)
        item_ref[g, 0] = lax.dot_general(
            residual, chosen, (((0,), (0,)), ((), ())), preferred_element_type=jnp.float32
        )
        terms = jnp.dot(residual, v, preferred_element_type=jnp.float32)
        for s, b in enumerate(chosen_rows):
            region_ref[b] += terms[s * block:(s + 1) * block]

    if last:
        @pl.when(step == pl.num_programs(0) - 1)
        def _():
            wide = u_ref[...].astype(jnp.float32)
            region_ref[...] = wide - region_rate * (region_ref[...] + decay_rate * wide)


def local_grads(region_blocks, panels, tiles, rows_flat, counts, core_sel, region_in, last):
    row_blocks, block, width = region_blocks.shape
    ny, nzl = panels.shape[:2]
    slots = tiles.shape[1]
    pairs = ny // 2
    first = region_in is None

    def slab_map(g):
        return lambda i, r, c, s: (((i // pairs) * ny + 2 * (i % pairs) + g) * 2 + s[0], 0, 0, 0)

    in_specs = [
        pl.BlockSpec((row_blocks, block, width), lambda i, r, c, s: (0, 0, 0)),
        pl.BlockSpec((2, 1, block, width), lambda i, r, c, s: (i % pairs, i // pairs, 0, 0)),
        pl.BlockSpec((1, slots, block, block), slab_map(0)),
        pl.BlockSpec((1, slots, block, block), slab_map(1)),
    ]
    operands = [region_blocks, panels, tiles, tiles]
    aliases = {}
    if not first:
        in_specs.append(pl.BlockSpec((row_blocks, block, width), lambda i, r, c, s: (0, 0, 0)))
        operands.append(region_in)
        aliases = {3 + len(operands) - 1: 0}
    grid_spec = pltpu.PrefetchScalarGridSpec(
        num_scalar_prefetch=3,
        grid=(ny * nzl // 2,),
        in_specs=in_specs,
        out_specs=[
            pl.BlockSpec((row_blocks, block, width), lambda i, r, c, s: (0, 0, 0)),
            pl.BlockSpec((2, 1, block, width), lambda i, r, c, s: (i % pairs, i // pairs, 0, 0)),
        ],
    )
    n_panels = ny * nzl
    flops = 3 * 2 * n_panels * slots * block * block * width
    bytes_accessed = (
        region_blocks.size * 2 + panels.size * 2 + n_panels * slots * block * block * 2
        + region_blocks.size * 8 + panels.size * 4
    )
    return pl.pallas_call(
        functools.partial(grad_kernel, first, last, ny),
        grid_spec=grid_spec,
        out_shape=[
            jax.ShapeDtypeStruct((row_blocks, block, width), jnp.float32),
            jax.ShapeDtypeStruct((ny, nzl, block, width), jnp.float32),
        ],
        input_output_aliases=aliases,
        compiler_params=pltpu.CompilerParams(
            dimension_semantics=("arbitrary",),
            vmem_limit_bytes=48 * 1024 * 1024,
        ),
        cost_estimate=pl.CostEstimate(
            flops=flops, bytes_accessed=bytes_accessed, transcendentals=0
        ),
    )(rows_flat, counts, core_sel, *operands)


def take(arr, index):
    return lax.dynamic_index_in_dim(arr, index, 0, keepdims=False)


def put(arr, value, index):
    return lax.dynamic_update_index_in_dim(arr, value, index, 0)


def ring_pairs(n, step):
    return [(s, (s + step) % n) for s in range(n)]


def rings_reduce_scatter(jobs):
    state = []
    for x, axes, n in jobs:
        me = lax.axis_index(axes)
        half = x.shape[1] // 2
        ahead, behind = x[:, :half], x[:, half:]
        state.append([ahead, behind, axes, n, me, take(ahead, (me - 1) % n), take(behind, (me + 1) % n)])
    for t in range(max(job[2] for job in jobs) - 1):
        for st in state:
            ahead, behind, axes, n, me, acc_a, acc_b = st
            if t >= n - 1:
                continue
            got_a = lax.ppermute(acc_a, axes, ring_pairs(n, 1))
            got_b = lax.ppermute(acc_b, axes, ring_pairs(n, n - 1))
            st[5] = got_a + take(ahead, (me - 2 - t) % n)
            st[6] = got_b + take(behind, (me + 2 + t) % n)
    return [jnp.concatenate([st[5], st[6]], axis=0) for st in state]


def rings_all_gather(jobs):
    state = []
    for x, axes, n in jobs:
        me = lax.axis_index(axes)
        half = x.shape[0] // 2
        cur_a, cur_b = x[:half], x[half:]
        buf_a = put(jnp.zeros((n,) + cur_a.shape, x.dtype), cur_a, me)
        buf_b = put(jnp.zeros((n,) + cur_b.shape, x.dtype), cur_b, me)
        state.append([axes, n, me, cur_a, cur_b, buf_a, buf_b])
    for t in range(max(job[2] for job in jobs) - 1):
        for st in state:
            axes, n, me, cur_a, cur_b, buf_a, buf_b = st
            if t >= n - 1:
                continue
            cur_a = lax.ppermute(cur_a, axes, ring_pairs(n, 1))
            cur_b = lax.ppermute(cur_b, axes, ring_pairs(n, n - 1))
            st[3], st[4] = cur_a, cur_b
            st[5] = put(buf_a, cur_a, (me - 1 - t) % n)
            st[6] = put(buf_b, cur_b, (me + 1 + t) % n)
    return [jnp.concatenate([st[5], st[6]], axis=1) for st in state]


def direct_reduce_scatter(jobs):
    outs = []
    for x, axes, n in jobs:
        me = lax.axis_index(axes)
        total = take(x, me)
        for k in range(1, n):
            total = total + lax.ppermute(take(x, (me + k) % n), axes, ring_pairs(n, k))
        outs.append(total)
    return outs


def direct_all_gather(jobs):
    outs = []
    for x, axes, n in jobs:
        me = lax.axis_index(axes)
        buf = put(jnp.zeros((n,) + x.shape, x.dtype), x, me)
        for k in range(1, n):
            buf = put(buf, lax.ppermute(x, axes, ring_pairs(n, k)), (me - k) % n)
        outs.append(buf)
    return outs


def on_device(region_factors, item_factors, slab_blocks, block_rows, counts):
    n_zh, n_x = lax.axis_size("zh"), lax.axis_size("x")
    n_zl, n_y, n_core = lax.axis_size("zl"), lax.axis_size("y"), lax.axis_size("core")
    block = slab_blocks.shape[-1]
    width = region_factors.shape[-1]
    jj = block // (n_zh * n_x)
    hw = width // 2
    row_blocks = region_factors.shape[0] // block
    region_blocks = region_factors.reshape(row_blocks, block, width)

    piece = item_factors[0]
    (got,) = direct_all_gather([(piece, "zh", n_zh)])
    (got,) = direct_all_gather([(got, "zl", n_zl)])
    part_a, part_b = direct_all_gather([(got[..., :hw], "x", n_x), (got[..., hw:], "y", n_y)])
    part_a, part_b = direct_all_gather([(part_a, "y", n_y), (part_b, "x", n_x)])
    part_a = part_a.transpose(0, 2, 3, 1, 4, 5)
    part_b = part_b.transpose(1, 2, 3, 0, 4, 5)
    panel_y = jnp.concatenate([part_a, part_b], axis=-1).reshape(n_y, n_zl, block, width)
    swap = ring_pairs(n_core, 1)
    panel_other = lax.ppermute(panel_y, "core", swap)

    me = lax.axis_index("core")
    tiles, rows_flat, live = slab_blocks[0], block_rows[0].reshape(-1), counts[0]
    partial_regions, other_part = local_grads(
        region_blocks, panel_other, tiles, rows_flat, live, (1 - me)[None], None, False
    )
    got = lax.ppermute(other_part, "core", swap)
    new_regions, own_part = local_grads(
        region_blocks, panel_y, tiles, rows_flat, live, me[None], partial_regions, True
    )

    grad = own_part + got
    grad = grad.reshape(n_y, n_zl, n_zh, n_x, jj, width)
    part_a = grad[..., :hw]
    part_b = grad[..., hw:].transpose(3, 0, 1, 2, 4, 5)
    part_a, part_b = rings_reduce_scatter([(part_a, "y", n_y), (part_b, "x", n_x)])
    part_a = part_a.transpose(2, 0, 1, 3, 4)
    part_a, part_b = direct_reduce_scatter([(part_a, "x", n_x), (part_b, "y", n_y)])
    grad = jnp.concatenate([part_a, part_b], axis=-1)
    (grad,) = direct_reduce_scatter([(grad, "zl", n_zl)])
    (own_grad,) = direct_reduce_scatter([(grad, "zh", n_zh)])

    own_rows = piece.astype(jnp.float32)
    new_items = own_rows - item_rate * (own_grad + decay_rate * own_rows)
    return (new_regions.reshape(row_blocks * block, width), new_items[None])


def solution(mesh):
    rows, cols = mesh.devices.shape
    n_zh = 2
    n_core = 2
    n_x = rows // n_zh
    n_y = 4
    n_zl = cols // (n_y * n_core)
    fine = Mesh(mesh.devices.reshape(n_zh, n_x, n_zl, n_y, n_core), AXES)
    return jax.shard_map(
        on_device,
        mesh=fine,
        in_specs=(
            P(AXES, None),
            P(("zl", "y", "core"), ("zh", "x"), None),
            P(AXES, None, None, None, None),
            P(AXES, None, None),
            P(AXES, None),
        ),
        out_specs=(P(AXES, None), P(("zl", "y", "core"), ("zh", "x"), None)),
        check_vma=False,
    )
```

profile of v0, /device:TPU:32, one launch (start us, length us, event | category | flops | bytes accessed | tf_op | source)
XLA Modules:
  0.0 157.5 jit_solution(11814996698189097789)
XLA Ops:
  0.6 6.4 %collective-permute-start = (bf16[16,512]{1,0:T(8,128)(2,1)}, bf16[16,512]{1,0:T(8,128)(2,1)S(1)}, u32[]{:S(2)}, u32[]{:S(2)}) collective-permute-start(bf16[16,512]{1,0:T(8,128)(2,1)} %bitcast.164), channel_id=1, source_target_pairs={{0,128},{128,0},{1,129},{129,1},{2,130},{130,2},{3,131},{131,3},{4... | collective-permute-start | bytes 49160 | tf_op jit(solution)/shard_map/ppermute | solution.py:188
  8.9 1.6 collective-permute-start.1
  10.5 2.3 %collective-permute-start.2 = (bf16[2,16,512]{2,1,0:T(8,128)(2,1)S(1)}, bf16[2,16,512]{2,1,0:T(8,128)(2,1)S(1)}, u32[]{:S(2)}, u32[]{:S(2)}) collective-permute-start(bf16[2,16,512]{2,1,0:T(8,128)(2,1)S(1)} %bitcast_dynamic-update-slice_fusion.20), channel_id=1, source_target_pairs={{0,16},{8,24},{16,0},{24,8},{1,17},{9,25},{17,1},{25,9},{2,18},{10... | collective-permute-start | bytes 98312 | tf_op jit(solution)/shard_map/ppermute | solution.py:188
  17.8 2.7 %collective-permute-start.5 = (bf16[4,2,16,256]{3,2,1,0:T(8,128)(2,1)S(1)}, bf16[4,2,16,256]{3,2,1,0:T(8,128)(2,1)S(1)}, u32[]{:S(2)}, u32[]{:S(2)}) collective-permute-start(bf16[4,2,16,256]{3,2,1,0:T(8,128)(2,1)S(1)} %get-tuple-element.23), channel_id=1, source_target_pairs={{0,64},{32,96},{64,0},{96,32},{1,65},{33,97},{65,1},{97,33},{2,66}... | collective-permute-start | bytes 196616 | tf_op jit(solution)/shard_map/ppermute | solution.py:188
  20.5 1.4 collective-permute-start.6
  22.0 1.6 %collective-permute-start.10 = (bf16[4,2,16,256]{3,2,1,0:T(8,128)(2,1)S(1)}, bf16[4,2,16,256]{3,2,1,0:T(8,128)(2,1)S(1)}, u32[]{:S(2)}, u32[]{:S(2)}) collective-permute-start(bf16[4,2,16,256]{3,2,1,0:T(8,128)(2,1)S(1)} %get-tuple-element.24), channel_id=1, source_target_pairs={{0,2},{2,4},{4,6},{6,0},{1,3},{3,5},{5,7},{7,1},{8,10},{10,12},{12... | collective-permute-start | bytes 196616 | tf_op jit(solution)/shard_map/ppermute | solution.py:188
  23.6 2.9 %collective-permute-start.11 = (bf16[4,2,16,256]{3,2,1,0:T(8,128)(2,1)S(1)}, bf16[4,2,16,256]{3,2,1,0:T(8,128)(2,1)S(1)}, u32[]{:S(2)}, u32[]{:S(2)}) collective-permute-start(bf16[4,2,16,256]{3,2,1,0:T(8,128)(2,1)S(1)} %get-tuple-element.24), channel_id=1, source_target_pairs={{0,4},{2,6},{4,0},{6,2},{1,5},{3,7},{5,1},{7,3},{8,12},{10,14},{12... | collective-permute-start | bytes 196616 | tf_op jit(solution)/shard_map/ppermute | solution.py:188
  29.6 2.0 %collective-permute-start.9 = (bf16[4,4,2,16,256]{4,3,2,1,0:T(8,128)(2,1)S(1)}, bf16[4,4,2,16,256]{4,3,2,1,0:T(8,128)(2,1)S(1)}, u32[]{:S(2)}, u32[]{:S(2)}) collective-permute-start(bf16[4,4,2,16,256]{4,3,2,1,0:T(8,128)(2,1)S(1)} %bitcast_dynamic-update-slice_fusion.12), channel_id=1, source_target_pairs={{0,6},{2,0},{4,2},{6,4},{1,7},{3,1},{5,3},{7,5},{8,14},{10,8},{12,... | collective-permute-start | bytes 786440 | tf_op jit(solution)/shard_map/ppermute | solution.py:188
  32.4 2.6 %collective-permute-start.14 = (bf16[4,4,2,16,256]{4,3,2,1,0:T(8,128)(2,1)S(1)}, bf16[4,4,2,16,256]{4,3,2,1,0:T(8,128)(2,1)S(1)}, u32[]{:S(2)}, u32[]{:S(2)}) collective-permute-start(bf16[4,4,2,16,256]{4,3,2,1,0:T(8,128)(2,1)S(1)} %bitcast_dynamic-update-slice_fusion.8), channel_id=1, source_target_pairs={{0,64},{32,96},{64,0},{96,32},{1,65},{33,97},{65,1},{97,33},{2,66}... | collective-permute-start | bytes 786440 | tf_op jit(solution)/shard_map/ppermute | solution.py:188
  35.3 4.2 %collective-permute-done.7 = bf16[4,4,2,16,256]{4,3,2,1,0:T(8,128)(2,1)S(1)} collective-permute-done((bf16[4,4,2,16,256]{4,3,2,1,0:T(8,128)(2,1)S(1)}, bf16[4,4,2,16,256]{4,3,2,1,0:T(8,128)(2,1)S(1)}, u32[]{:S(2)}, u32[]{:S(2)}) %collective-permute-start.7) | collective-permute-done | bytes 262176 | tf_op jit(solution)/shard_map/ppermute | solution.py:188
  40.4 1.7 %collective-permute-done.14 = bf16[4,4,2,16,256]{4,3,2,1,0:T(8,128)(2,1)S(1)} collective-permute-done((bf16[4,4,2,16,256]{4,3,2,1,0:T(8,128)(2,1)S(1)}, bf16[4,4,2,16,256]{4,3,2,1,0:T(8,128)(2,1)S(1)}, u32[]{:S(2)}, u32[]{:S(2)}) %collective-permute-start.14) | collective-permute-done | bytes 262176 | tf_op jit(solution)/shard_map/ppermute | solution.py:188
  42.2 3.8 %collective-permute-done.15 = bf16[4,4,2,16,256]{4,3,2,1,0:T(8,128)(2,1)S(1)} collective-permute-done((bf16[4,4,2,16,256]{4,3,2,1,0:T(8,128)(2,1)S(1)}, bf16[4,4,2,16,256]{4,3,2,1,0:T(8,128)(2,1)S(1)}, u32[]{:S(2)}, u32[]{:S(2)}) %collective-permute-start.15) | collective-permute-done | bytes 262176 | tf_op jit(solution)/shard_map/ppermute | solution.py:188
  46.7 4.1 %collective-permute-done.16.v_ref = bf16[4,4,128,512]{3,2,1,0:T(8,128)(2,1)} collective-permute-done((bf16[4,4,128,512]{3,2,1,0:T(8,128)(2,1)S(1)}, bf16[4,4,128,512]{3,2,1,0:T(8,128)(2,1)}, u32[]{:S(2)}, u32[]{:S(2)}) %collective-permute-start.16) | collective-permute-done | bytes 2097184 | tf_op jit(solution)/shard_map/ppermute | solution.py:212
  50.8 20.0 %shard_map.68 = (f32[8,128,512]{2,1,0:T(8,128)}, f32[4,4,128,512]{3,2,1,0:T(8,128)}) custom-call(s32[192]{0:T(256)S(1)} %reshape_squeeze.3.rows_ref, s32[32]{0:T(128)S(1)} %bitcast.159, s32[1]{0:T(128)} %bitcast.36.sel_ref, bf16[8,128,512]{2,1,0:T(8,128)(2,1)S(1)} %bitcast.157, bf16[4,4,128,512]{3,2,1,0:T(8,128)(2,1)} %collective-permute-done.16.v_ref, ...), custom_call_target="tpu_custom_call" | custom-call | flops 4831838208 | bytes 14680064 | tf_op jit(solution)/shard_map/pallas_call | solution.py:100
  70.9 21.2 %shard_map.69 = (f32[8,128,512]{2,1,0:T(8,128)}, f32[4,4,128,512]{3,2,1,0:T(8,128)}) custom-call(s32[192]{0:T(256)S(1)} %reshape_squeeze.3.rows_ref, s32[32]{0:T(128)S(1)} %bitcast.160, s32[1]{0:T(128)} %bitcast.1.sel_ref, bf16[8,128,512]{2,1,0:T(8,128)(2,1)S(1)} %bitcast.158, ...), custom_call_target="tpu_custom_call", output_to_operand_aliasing={{0}: (7, {})} | custom-call | flops 4831838208 | bytes 14680064 | tf_op jit(solution)/shard_map/pallas_call | solution.py:100
  92.2 4.5 %add.376 = f32[4,4,128,512]{3,2,1,0:T(8,128)S(1)} add(f32[4,4,128,512]{3,2,1,0:T(8,128)} %get-tuple-element.8, f32[4,4,128,512]{3,2,1,0:T(8,128)} %collective-permute-done.17) | non-fusion elementwise | flops 1048576 | bytes 12582912 | tf_op jit(solution)/shard_map/add | solution.py:224
  101.9 4.2 %collective-permute-done.30 = f32[2,4,2,16,256]{4,3,2,1,0:T(8,128)S(1)} collective-permute-done((f32[2,4,2,16,256]{4,3,2,1,0:T(8,128)S(1)}, f32[2,4,2,16,256]{4,3,2,1,0:T(8,128)S(1)}, u32[]{:S(2)}, u32[]{:S(2)}) %collective-permute-start.30) | collective-permute-done | bytes 262176 | tf_op jit(solution)/shard_map/ppermute | solution.py:143
  106.2 2.5 %collective-permute-start.31 = (f32[2,4,2,16,256]{4,3,2,1,0:T(8,128)S(1)}, f32[2,4,2,16,256]{4,3,2,1,0:T(8,128)S(1)}, u32[]{:S(2)}, u32[]{:S(2)}) collective-permute-start(f32[2,4,2,16,256]{4,3,2,1,0:T(8,128)S(1)} %bitcast_add_fusion.2), channel_id=1, source_target_pairs={{0,96},{32,0},{64,32},{96,64},{1,97},{33,1},{65,33},{97,65},{2,98}... | collective-permute-start | bytes 786440 | tf_op jit(solution)/shard_map/ppermute | solution.py:143
  108.9 2.4 %collective-permute-start.22 = (f32[2,2,4,16,256]{4,3,2,1,0:T(8,128)S(1)}, f32[2,2,4,16,256]{4,3,2,1,0:T(8,128)S(1)}, u32[]{:S(2)}, u32[]{:S(2)}) collective-permute-start(f32[2,2,4,16,256]{4,3,2,1,0:T(8,128)S(1)} %bitcast_add_fusion.8), channel_id=1, source_target_pairs={{0,6},{2,0},{4,2},{6,4},{1,7},{3,1},{5,3},{7,5},{8,14},{10,8},{12,... | collective-permute-start | bytes 786440 | tf_op jit(solution)/shard_map/ppermute | solution.py:143
  111.5 2.6 %collective-permute-done.31 = f32[2,4,2,16,256]{4,3,2,1,0:T(8,128)S(1)} collective-permute-done((f32[2,4,2,16,256]{4,3,2,1,0:T(8,128)S(1)}, f32[2,4,2,16,256]{4,3,2,1,0:T(8,128)S(1)}, u32[]{:S(2)}, u32[]{:S(2)}) %collective-permute-start.31) | collective-permute-done | bytes 262176 | tf_op jit(solution)/shard_map/ppermute | solution.py:143
  114.1 3.7 %collective-permute-start.32 = (f32[2,4,2,16,256]{4,3,2,1,0:T(8,128)S(1)}, f32[2,4,2,16,256]{4,3,2,1,0:T(8,128)S(1)}, u32[]{:S(2)}, u32[]{:S(2)}) collective-permute-start(f32[2,4,2,16,256]{4,3,2,1,0:T(8,128)S(1)} %bitcast_add_fusion.1), channel_id=1, source_target_pairs={{0,96},{32,0},{64,32},{96,64},{1,97},{33,1},{65,33},{97,65},{2,98}... | collective-permute-start | bytes 786440 | tf_op jit(solution)/shard_map/ppermute | solution.py:143
  118.0 2.2 %collective-permute-start.23 = (f32[2,2,4,16,256]{4,3,2,1,0:T(8,128)S(1)}, f32[2,2,4,16,256]{4,3,2,1,0:T(8,128)S(1)}, u32[]{:S(2)}, u32[]{:S(2)}) collective-permute-start(f32[2,2,4,16,256]{4,3,2,1,0:T(8,128)S(1)} %bitcast_add_fusion.7), channel_id=1, source_target_pairs={{0,6},{2,0},{4,2},{6,4},{1,7},{3,1},{5,3},{7,5},{8,14},{10,8},{12,... | collective-permute-start | bytes 786440 | tf_op jit(solution)/shard_map/ppermute | solution.py:143
  120.4 1.8 %collective-permute-done.32 = f32[2,4,2,16,256]{4,3,2,1,0:T(8,128)S(1)} collective-permute-done((f32[2,4,2,16,256]{4,3,2,1,0:T(8,128)S(1)}, f32[2,4,2,16,256]{4,3,2,1,0:T(8,128)S(1)}, u32[]{:S(2)}, u32[]{:S(2)}) %collective-permute-start.32) | collective-permute-done | bytes 262176 | tf_op jit(solution)/shard_map/ppermute | solution.py:143
  122.2 3.5 %collective-permute-done.29 = f32[2,4,2,16,256]{4,3,2,1,0:T(8,128)S(1)} collective-permute-done((f32[2,4,2,16,256]{4,3,2,1,0:T(8,128)S(1)}, f32[2,4,2,16,256]{4,3,2,1,0:T(8,128)S(1)}, u32[]{:S(2)}, u32[]{:S(2)}) %collective-permute-start.29) | collective-permute-done | bytes 262176 | tf_op jit(solution)/shard_map/ppermute | solution.py:142
  126.3 3.3 %collective-permute-start.34 = (f32[4,2,16,256]{3,2,1,0:T(8,128)S(1)}, f32[4,2,16,256]{3,2,1,0:T(8,128)S(1)}, u32[]{:S(2)}, u32[]{:S(2)}) collective-permute-start(f32[4,2,16,256]{3,2,1,0:T(8,128)S(1)} %get-tuple-element.15), channel_id=1, source_target_pairs={{0,4},{2,6},{4,0},{6,2},{1,5},{3,7},{5,1},{7,3},{8,12},{10,14},{12... | collective-permute-start | bytes 393224 | tf_op jit(solution)/shard_map/ppermute | solution.py:177
  130.0 5.2 %collective-permute-start.25 = (f32[4,2,16,256]{3,2,1,0:T(8,128)S(1)}, f32[4,2,16,256]{3,2,1,0:T(8,128)S(1)}, u32[]{:S(2)}, u32[]{:S(2)}) collective-permute-start(f32[4,2,16,256]{3,2,1,0:T(8,128)S(1)} %get-tuple-element.18), channel_id=1, source_target_pairs={{0,64},{32,96},{64,0},{96,32},{1,65},{33,97},{65,1},{97,33},{2,66}... | collective-permute-start | bytes 393224 | tf_op jit(solution)/shard_map/ppermute | solution.py:177
  136.7 2.9 %collective-permute-done.25 = f32[4,2,16,256]{3,2,1,0:T(8,128)S(1)} collective-permute-done((f32[4,2,16,256]{3,2,1,0:T(8,128)S(1)}, f32[4,2,16,256]{3,2,1,0:T(8,128)S(1)}, u32[]{:S(2)}, u32[]{:S(2)}) %collective-permute-start.25) | collective-permute-done | bytes 131104 | tf_op jit(solution)/shard_map/ppermute | solution.py:177
  141.4 2.9 %collective-permute-start.37 = (f32[2,16,512]{2,1,0:T(8,128)S(1)}, f32[2,16,512]{2,1,0:T(8,128)S(1)}, u32[]{:S(2)}, u32[]{:S(2)}) collective-permute-start(f32[2,16,512]{2,1,0:T(8,128)S(1)} %get-tuple-element.21), channel_id=1, source_target_pairs={{0,16},{8,24},{16,0},{24,8},{1,17},{9,25},{17,1},{25,9},{2,18},{10... | collective-permute-start | bytes 196616 | tf_op jit(solution)/shard_map/ppermute | solution.py:177
  145.3 2.0 %collective-permute-done.37 = f32[2,16,512]{2,1,0:T(8,128)S(1)} collective-permute-done((f32[2,16,512]{2,1,0:T(8,128)S(1)}, f32[2,16,512]{2,1,0:T(8,128)S(1)}, u32[]{:S(2)}, u32[]{:S(2)}) %collective-permute-start.37) | collective-permute-done | bytes 65568 | tf_op jit(solution)/shard_map/ppermute | solution.py:177
  147.3 1.6 collective-permute-done.38
  148.9 5.2 %collective-permute-start.39 = (f32[16,512]{1,0:T(8,128)S(1)}, f32[16,512]{1,0:T(8,128)S(1)}, u32[]{:S(2)}, u32[]{:S(2)}) collective-permute-start(f32[16,512]{1,0:T(8,128)S(1)} %dynamic-slice_bitcast_fusion.4), channel_id=1, source_target_pairs={{0,128},{128,0},{1,129},{129,1},{2,130},{130,2},{3,131},{131,3},{4... | collective-permute-start | bytes 98312 | tf_op jit(solution)/shard_map/ppermute | solution.py:177
  154.1 2.7 %collective-permute-done.39 = f32[16,512]{1,0:T(8,128)S(1)} collective-permute-done((f32[16,512]{1,0:T(8,128)S(1)}, f32[16,512]{1,0:T(8,128)S(1)}, u32[]{:S(2)}, u32[]{:S(2)}) %collective-permute-start.39) | collective-permute-done | bytes 32800 | tf_op jit(solution)/shard_map/ppermute | solution.py:177
  (118 shorter events, 24.7 us)
Async XLA Ops:
  0.6 8.3 %collective-permute-start = (bf16[16,512]{1,0:T(8,128)(2,1)}, bf16[16,512]{1,0:T(8,128)(2,1)S(1)}, u32[]{:S(2)}, u32[]{:S(2)}) collective-permute-start(bf16[16,512]{1,0:T(8,128)(2,1)} %bitcast.164), channel_id=1, source_target_pairs={{0,128},{128,0},{1,129},{129,1},{2,130},{130,2},{3,131},{131,3},{4... | collective-permute-start | bytes 49160 | tf_op jit(solution)/shard_map/ppermute | solution.py:188
  16.7 9.8 %collective-permute-start.4 = (bf16[4,2,16,256]{3,2,1,0:T(8,128)(2,1)S(1)}, bf16[4,2,16,256]{3,2,1,0:T(8,128)(2,1)S(1)}, u32[]{:S(2)}, u32[]{:S(2)}) collective-permute-start(bf16[4,2,16,256]{3,2,1,0:T(8,128)(2,1)S(1)} %get-tuple-element.23), channel_id=1, source_target_pairs={{0,32},{32,64},{64,96},{96,0},{1,33},{33,65},{65,97},{97,1},{2,34}... | collective-permute-start | bytes 196616 | tf_op jit(solution)/shard_map/ppermute | solution.py:188
  17.8 10.2 %collective-permute-start.5 = (bf16[4,2,16,256]{3,2,1,0:T(8,128)(2,1)S(1)}, bf16[4,2,16,256]{3,2,1,0:T(8,128)(2,1)S(1)}, u32[]{:S(2)}, u32[]{:S(2)}) collective-permute-start(bf16[4,2,16,256]{3,2,1,0:T(8,128)(2,1)S(1)} %get-tuple-element.23), channel_id=1, source_target_pairs={{0,64},{32,96},{64,0},{96,32},{1,65},{33,97},{65,1},{97,33},{2,66}... | collective-permute-start | bytes 196616 | tf_op jit(solution)/shard_map/ppermute | solution.py:188
  20.5 7.5 %collective-permute-start.6 = (bf16[4,2,16,256]{3,2,1,0:T(8,128)(2,1)S(1)}, bf16[4,2,16,256]{3,2,1,0:T(8,128)(2,1)S(1)}, u32[]{:S(2)}, u32[]{:S(2)}) collective-permute-start(bf16[4,2,16,256]{3,2,1,0:T(8,128)(2,1)S(1)} %get-tuple-element.23), channel_id=1, source_target_pairs={{0,96},{32,0},{64,32},{96,64},{1,97},{33,1},{65,33},{97,65},{2,98}... | collective-permute-start | bytes 196616 | tf_op jit(solution)/shard_map/ppermute | solution.py:188
  22.0 7.6 %collective-permute-start.10 = (bf16[4,2,16,256]{3,2,1,0:T(8,128)(2,1)S(1)}, bf16[4,2,16,256]{3,2,1,0:T(8,128)(2,1)S(1)}, u32[]{:S(2)}, u32[]{:S(2)}) collective-permute-start(bf16[4,2,16,256]{3,2,1,0:T(8,128)(2,1)S(1)} %get-tuple-element.24), channel_id=1, source_target_pairs={{0,2},{2,4},{4,6},{6,0},{1,3},{3,5},{5,7},{7,1},{8,10},{10,12},{12... | collective-permute-start | bytes 196616 | tf_op jit(solution)/shard_map/ppermute | solution.py:188
  23.6 8.0 %collective-permute-start.11 = (bf16[4,2,16,256]{3,2,1,0:T(8,128)(2,1)S(1)}, bf16[4,2,16,256]{3,2,1,0:T(8,128)(2,1)S(1)}, u32[]{:S(2)}, u32[]{:S(2)}) collective-permute-start(bf16[4,2,16,256]{3,2,1,0:T(8,128)(2,1)S(1)} %get-tuple-element.24), channel_id=1, source_target_pairs={{0,4},{2,6},{4,0},{6,2},{1,5},{3,7},{5,1},{7,3},{8,12},{10,14},{12... | collective-permute-start | bytes 196616 | tf_op jit(solution)/shard_map/ppermute | solution.py:188
  28.1 11.5 %collective-permute-start.7 = (bf16[4,4,2,16,256]{4,3,2,1,0:T(8,128)(2,1)S(1)}, bf16[4,4,2,16,256]{4,3,2,1,0:T(8,128)(2,1)S(1)}, u32[]{:S(2)}, u32[]{:S(2)}) collective-permute-start(bf16[4,4,2,16,256]{4,3,2,1,0:T(8,128)(2,1)S(1)} %bitcast_dynamic-update-slice_fusion.12), channel_id=1, source_target_pairs={{0,2},{2,4},{4,6},{6,0},{1,3},{3,5},{5,7},{7,1},{8,10},{10,12},{12... | collective-permute-start | bytes 786440 | tf_op jit(solution)/shard_map/ppermute | solution.py:188
  28.8 10.8 %collective-permute-start.8 = (bf16[4,4,2,16,256]{4,3,2,1,0:T(8,128)(2,1)S(1)}, bf16[4,4,2,16,256]{4,3,2,1,0:T(8,128)(2,1)S(1)}, u32[]{:S(2)}, u32[]{:S(2)}) collective-permute-start(bf16[4,4,2,16,256]{4,3,2,1,0:T(8,128)(2,1)S(1)} %bitcast_dynamic-update-slice_fusion.12), channel_id=1, source_target_pairs={{0,4},{2,6},{4,0},{6,2},{1,5},{3,7},{5,1},{7,3},{8,12},{10,14},{12... | collective-permute-start | bytes 786440 | tf_op jit(solution)/shard_map/ppermute | solution.py:188
  29.6 10.7 %collective-permute-start.9 = (bf16[4,4,2,16,256]{4,3,2,1,0:T(8,128)(2,1)S(1)}, bf16[4,4,2,16,256]{4,3,2,1,0:T(8,128)(2,1)S(1)}, u32[]{:S(2)}, u32[]{:S(2)}) collective-permute-start(bf16[4,4,2,16,256]{4,3,2,1,0:T(8,128)(2,1)S(1)} %bitcast_dynamic-update-slice_fusion.12), channel_id=1, source_target_pairs={{0,6},{2,0},{4,2},{6,4},{1,7},{3,1},{5,3},{7,5},{8,14},{10,8},{12,... | collective-permute-start | bytes 786440 | tf_op jit(solution)/shard_map/ppermute | solution.py:188
  31.7 8.7 %collective-permute-start.13 = (bf16[4,4,2,16,256]{4,3,2,1,0:T(8,128)(2,1)S(1)}, bf16[4,4,2,16,256]{4,3,2,1,0:T(8,128)(2,1)S(1)}, u32[]{:S(2)}, u32[]{:S(2)}) collective-permute-start(bf16[4,4,2,16,256]{4,3,2,1,0:T(8,128)(2,1)S(1)} %bitcast_dynamic-update-slice_fusion.8), channel_id=1, source_target_pairs={{0,32},{32,64},{64,96},{96,0},{1,33},{33,65},{65,97},{97,1},{2,34}... | collective-permute-start | bytes 786440 | tf_op jit(solution)/shard_map/ppermute | solution.py:188
  32.4 9.8 %collective-permute-start.14 = (bf16[4,4,2,16,256]{4,3,2,1,0:T(8,128)(2,1)S(1)}, bf16[4,4,2,16,256]{4,3,2,1,0:T(8,128)(2,1)S(1)}, u32[]{:S(2)}, u32[]{:S(2)}) collective-permute-start(bf16[4,4,2,16,256]{4,3,2,1,0:T(8,128)(2,1)S(1)} %bitcast_dynamic-update-slice_fusion.8), channel_id=1, source_target_pairs={{0,64},{32,96},{64,0},{96,32},{1,65},{33,97},{65,1},{97,33},{2,66}... | collective-permute-start | bytes 786440 | tf_op jit(solution)/shard_map/ppermute | solution.py:188
  39.6 6.4 %collective-permute-start.15 = (bf16[4,4,2,16,256]{4,3,2,1,0:T(8,128)(2,1)S(1)}, bf16[4,4,2,16,256]{4,3,2,1,0:T(8,128)(2,1)S(1)}, u32[]{:S(2)}, u32[]{:S(2)}) collective-permute-start(bf16[4,4,2,16,256]{4,3,2,1,0:T(8,128)(2,1)S(1)} %bitcast_dynamic-update-slice_fusion.8), channel_id=1, source_target_pairs={{0,96},{32,0},{64,32},{96,64},{1,97},{33,1},{65,33},{97,65},{2,98}... | collective-permute-start | bytes 786440 | tf_op jit(solution)/shard_map/ppermute | solution.py:188
  70.8 21.4 %collective-permute-start.17 = (f32[4,4,128,512]{3,2,1,0:T(8,128)}, f32[4,4,128,512]{3,2,1,0:T(8,128)}, u32[]{:S(2)}, u32[]{:S(2)}) collective-permute-start(f32[4,4,128,512]{3,2,1,0:T(8,128)} %get-tuple-element.9), channel_id=1, source_target_pairs={{0,1},{1,0},{2,3},{3,2},{4,5},{5,4},{6,7},{7,6},{8,9},{9,8},{10,11... | collective-permute-start | bytes 12582920 | tf_op jit(solution)/shard_map/ppermute | solution.py:219
  97.5 8.7 %collective-permute-start.30 = (f32[2,4,2,16,256]{4,3,2,1,0:T(8,128)S(1)}, f32[2,4,2,16,256]{4,3,2,1,0:T(8,128)S(1)}, u32[]{:S(2)}, u32[]{:S(2)}) collective-permute-start(f32[2,4,2,16,256]{4,3,2,1,0:T(8,128)S(1)} %dynamic-slice_bitcast_fusion), channel_id=1, source_target_pairs={{0,96},{32,0},{64,32},{96,64},{1,97},{33,1},{65,33},{97,65},{2,98}... | collective-permute-start | bytes 786440 | tf_op jit(solution)/shard_map/ppermute | solution.py:143
  98.8 9.9 %collective-permute-start.27 = (f32[2,4,2,16,256]{4,3,2,1,0:T(8,128)S(1)}, f32[2,4,2,16,256]{4,3,2,1,0:T(8,128)S(1)}, u32[]{:S(2)}, u32[]{:S(2)}) collective-permute-start(f32[2,4,2,16,256]{4,3,2,1,0:T(8,128)S(1)} %dynamic-slice_bitcast_fusion.1), channel_id=1, source_target_pairs={{0,32},{32,64},{64,96},{96,0},{1,33},{33,65},{65,97},{97,1},{2,34}... | collective-permute-start | bytes 786440 | tf_op jit(solution)/shard_map/ppermute | solution.py:142
  99.7 9.1 %collective-permute-start.21 = (f32[2,2,4,16,256]{4,3,2,1,0:T(8,128)S(1)}, f32[2,2,4,16,256]{4,3,2,1,0:T(8,128)S(1)}, u32[]{:S(2)}, u32[]{:S(2)}) collective-permute-start(f32[2,2,4,16,256]{4,3,2,1,0:T(8,128)S(1)} %dynamic-slice_bitcast_fusion.2), channel_id=1, source_target_pairs={{0,6},{2,0},{4,2},{6,4},{1,7},{3,1},{5,3},{7,5},{8,14},{10,8},{12,... | collective-permute-start | bytes 786440 | tf_op jit(solution)/shard_map/ppermute | solution.py:143
  101.2 10.2 %collective-permute-start.18 = (f32[2,2,4,16,256]{4,3,2,1,0:T(8,128)S(1)}, f32[2,2,4,16,256]{4,3,2,1,0:T(8,128)S(1)}, u32[]{:S(2)}, u32[]{:S(2)}) collective-permute-start(f32[2,2,4,16,256]{4,3,2,1,0:T(8,128)S(1)} %dynamic-slice_bitcast_fusion.3), channel_id=1, source_target_pairs={{0,2},{2,4},{4,6},{6,0},{1,3},{3,5},{5,7},{7,1},{8,10},{10,12},{12... | collective-permute-start | bytes 786440 | tf_op jit(solution)/shard_map/ppermute | solution.py:142
  106.2 7.8 %collective-permute-start.31 = (f32[2,4,2,16,256]{4,3,2,1,0:T(8,128)S(1)}, f32[2,4,2,16,256]{4,3,2,1,0:T(8,128)S(1)}, u32[]{:S(2)}, u32[]{:S(2)}) collective-permute-start(f32[2,4,2,16,256]{4,3,2,1,0:T(8,128)S(1)} %bitcast_add_fusion.2), channel_id=1, source_target_pairs={{0,96},{32,0},{64,32},{96,64},{1,97},{33,1},{65,33},{97,65},{2,98}... | collective-permute-start | bytes 786440 | tf_op jit(solution)/shard_map/ppermute | solution.py:143
  108.7 9.1 %collective-permute-start.28 = (f32[2,4,2,16,256]{4,3,2,1,0:T(8,128)S(1)}, f32[2,4,2,16,256]{4,3,2,1,0:T(8,128)S(1)}, u32[]{:S(2)}, u32[]{:S(2)}) collective-permute-start(f32[2,4,2,16,256]{4,3,2,1,0:T(8,128)S(1)} %bitcast_add_fusion.5), channel_id=1, source_target_pairs={{0,32},{32,64},{64,96},{96,0},{1,33},{33,65},{65,97},{97,1},{2,34}... | collective-permute-start | bytes 786440 | tf_op jit(solution)/shard_map/ppermute | solution.py:142
  108.9 9.0 %collective-permute-start.22 = (f32[2,2,4,16,256]{4,3,2,1,0:T(8,128)S(1)}, f32[2,2,4,16,256]{4,3,2,1,0:T(8,128)S(1)}, u32[]{:S(2)}, u32[]{:S(2)}) collective-permute-start(f32[2,2,4,16,256]{4,3,2,1,0:T(8,128)S(1)} %bitcast_add_fusion.8), channel_id=1, source_target_pairs={{0,6},{2,0},{4,2},{6,4},{1,7},{3,1},{5,3},{7,5},{8,14},{10,8},{12,... | collective-permute-start | bytes 786440 | tf_op jit(solution)/shard_map/ppermute | solution.py:143
  111.4 8.8 %collective-permute-start.19 = (f32[2,2,4,16,256]{4,3,2,1,0:T(8,128)S(1)}, f32[2,2,4,16,256]{4,3,2,1,0:T(8,128)S(1)}, u32[]{:S(2)}, u32[]{:S(2)}) collective-permute-start(f32[2,2,4,16,256]{4,3,2,1,0:T(8,128)S(1)} %bitcast_add_fusion.11), channel_id=1, source_target_pairs={{0,2},{2,4},{4,6},{6,0},{1,3},{3,5},{5,7},{7,1},{8,10},{10,12},{12... | collective-permute-start | bytes 786440 | tf_op jit(solution)/shard_map/ppermute | solution.py:142
  114.1 8.1 %collective-permute-start.32 = (f32[2,4,2,16,256]{4,3,2,1,0:T(8,128)S(1)}, f32[2,4,2,16,256]{4,3,2,1,0:T(8,128)S(1)}, u32[]{:S(2)}, u32[]{:S(2)}) collective-permute-start(f32[2,4,2,16,256]{4,3,2,1,0:T(8,128)S(1)} %bitcast_add_fusion.1), channel_id=1, source_target_pairs={{0,96},{32,0},{64,32},{96,64},{1,97},{33,1},{65,33},{97,65},{2,98}... | collective-permute-start | bytes 786440 | tf_op jit(solution)/shard_map/ppermute | solution.py:143
  117.8 7.9 %collective-permute-start.29 = (f32[2,4,2,16,256]{4,3,2,1,0:T(8,128)S(1)}, f32[2,4,2,16,256]{4,3,2,1,0:T(8,128)S(1)}, u32[]{:S(2)}, u32[]{:S(2)}) collective-permute-start(f32[2,4,2,16,256]{4,3,2,1,0:T(8,128)S(1)} %bitcast_add_fusion.4), channel_id=1, source_target_pairs={{0,32},{32,64},{64,96},{96,0},{1,33},{33,65},{65,97},{97,1},{2,34}... | collective-permute-start | bytes 786440 | tf_op jit(solution)/shard_map/ppermute | solution.py:142
  118.0 11.8 %collective-permute-start.23 = (f32[2,2,4,16,256]{4,3,2,1,0:T(8,128)S(1)}, f32[2,2,4,16,256]{4,3,2,1,0:T(8,128)S(1)}, u32[]{:S(2)}, u32[]{:S(2)}) collective-permute-start(f32[2,2,4,16,256]{4,3,2,1,0:T(8,128)S(1)} %bitcast_add_fusion.7), channel_id=1, source_target_pairs={{0,6},{2,0},{4,2},{6,4},{1,7},{3,1},{5,3},{7,5},{8,14},{10,8},{12,... | collective-permute-start | bytes 786440 | tf_op jit(solution)/shard_map/ppermute | solution.py:143
  120.3 9.6 %collective-permute-start.20 = (f32[2,2,4,16,256]{4,3,2,1,0:T(8,128)S(1)}, f32[2,2,4,16,256]{4,3,2,1,0:T(8,128)S(1)}, u32[]{:S(2)}, u32[]{:S(2)}) collective-permute-start(f32[2,2,4,16,256]{4,3,2,1,0:T(8,128)S(1)} %bitcast_add_fusion.10), channel_id=1, source_target_pairs={{0,2},{2,4},{4,6},{6,0},{1,3},{3,5},{5,7},{7,1},{8,10},{10,12},{12... | collective-permute-start | bytes 786440 | tf_op jit(solution)/shard_map/ppermute | solution.py:142
  125.8 9.4 %collective-permute-start.33 = (f32[4,2,16,256]{3,2,1,0:T(8,128)S(1)}, f32[4,2,16,256]{3,2,1,0:T(8,128)S(1)}, u32[]{:S(2)}, u32[]{:S(2)}) collective-permute-start(f32[4,2,16,256]{3,2,1,0:T(8,128)S(1)} %get-tuple-element.14), channel_id=1, source_target_pairs={{0,2},{2,4},{4,6},{6,0},{1,3},{3,5},{5,7},{7,1},{8,10},{10,12},{12... | collective-permute-start | bytes 393224 | tf_op jit(solution)/shard_map/ppermute | solution.py:177
  126.3 10.1 %collective-permute-start.34 = (f32[4,2,16,256]{3,2,1,0:T(8,128)S(1)}, f32[4,2,16,256]{3,2,1,0:T(8,128)S(1)}, u32[]{:S(2)}, u32[]{:S(2)}) collective-permute-start(f32[4,2,16,256]{3,2,1,0:T(8,128)S(1)} %get-tuple-element.15), channel_id=1, source_target_pairs={{0,4},{2,6},{4,0},{6,2},{1,5},{3,7},{5,1},{7,3},{8,12},{10,14},{12... | collective-permute-start | bytes 393224 | tf_op jit(solution)/shard_map/ppermute | solution.py:177
  129.5 6.9 %collective-permute-start.35 = (f32[4,2,16,256]{3,2,1,0:T(8,128)S(1)}, f32[4,2,16,256]{3,2,1,0:T(8,128)S(1)}, u32[]{:S(2)}, u32[]{:S(2)}) collective-permute-start(f32[4,2,16,256]{3,2,1,0:T(8,128)S(1)} %get-tuple-element.16), channel_id=1, source_target_pairs={{0,6},{2,0},{4,2},{6,4},{1,7},{3,1},{5,3},{7,5},{8,14},{10,8},{12,... | collective-permute-start | bytes 393224 | tf_op jit(solution)/shard_map/ppermute | solution.py:177
  129.9 6.8 %collective-permute-start.24 = (f32[4,2,16,256]{3,2,1,0:T(8,128)S(1)}, f32[4,2,16,256]{3,2,1,0:T(8,128)S(1)}, u32[]{:S(2)}, u32[]{:S(2)}) collective-permute-start(f32[4,2,16,256]{3,2,1,0:T(8,128)S(1)} %get-tuple-element.17), channel_id=1, source_target_pairs={{0,32},{32,64},{64,96},{96,0},{1,33},{33,65},{65,97},{97,1},{2,34}... | collective-permute-start | bytes 393224 | tf_op jit(solution)/shard_map/ppermute | solution.py:177
  130.0 9.5 %collective-permute-start.25 = (f32[4,2,16,256]{3,2,1,0:T(8,128)S(1)}, f32[4,2,16,256]{3,2,1,0:T(8,128)S(1)}, u32[]{:S(2)}, u32[]{:S(2)}) collective-permute-start(f32[4,2,16,256]{3,2,1,0:T(8,128)S(1)} %get-tuple-element.18), channel_id=1, source_target_pairs={{0,64},{32,96},{64,0},{96,32},{1,65},{33,97},{65,1},{97,33},{2,66}... | collective-permute-start | bytes 393224 | tf_op jit(solution)/shard_map/ppermute | solution.py:177
  141.4 5.9 %collective-permute-start.37 = (f32[2,16,512]{2,1,0:T(8,128)S(1)}, f32[2,16,512]{2,1,0:T(8,128)S(1)}, u32[]{:S(2)}, u32[]{:S(2)}) collective-permute-start(f32[2,16,512]{2,1,0:T(8,128)S(1)} %get-tuple-element.21), channel_id=1, source_target_pairs={{0,16},{8,24},{16,0},{24,8},{1,17},{9,25},{17,1},{25,9},{2,18},{10... | collective-permute-start | bytes 196616 | tf_op jit(solution)/shard_map/ppermute | solution.py:177
  148.9 7.9 %collective-permute-start.39 = (f32[16,512]{1,0:T(8,128)S(1)}, f32[16,512]{1,0:T(8,128)S(1)}, u32[]{:S(2)}, u32[]{:S(2)}) collective-permute-start(f32[16,512]{1,0:T(8,128)S(1)} %dynamic-slice_bitcast_fusion.4), channel_id=1, source_target_pairs={{0,128},{128,0},{1,129},{129,1},{2,130},{130,2},{3,131},{131,3},{4... | collective-permute-start | bytes 98312 | tf_op jit(solution)/shard_map/ppermute | solution.py:177
  (12 other events, 116.9 us)
where the time goes:
time: 158 us; the launch traced here: 157 us
  starting transfers between devices  65.9 us (42%)
  Pallas kernels  41.2 us (26%)
  waiting for transfers between devices  40.7 us (26%)
  other arithmetic  6.2 us (4%)
  local copies, waits for them, and re-layouts  2.43 us (2%)
    pallas_call x2, Pallas kernels, local_grads(): pl.pallas_call(functools.partial(grad_kernel, first, last, ny), grid_spec...  41.2 us
    ppermute x16, starting transfers between devices, direct_all_gather(): buf = put(buf, lax.ppermute(x, axes, ring_pairs(n, k)), (me - k) % n)  29.3 us
    ppermute x10, starting transfers between devices, direct_reduce_scatter(): total = total + lax.ppermute(take(x, (me + k) % n), axes, ring_pairs(n, k))  20.6 us
    ppermute x16, waiting for transfers between devices, direct_all_gather(): buf = put(buf, lax.ppermute(x, axes, ring_pairs(n, k)), (me - k) % n)  14.4 us
    ppermute x6, starting transfers between devices, rings_reduce_scatter(): got_b = lax.ppermute(acc_b, axes, ring_pairs(n, n - 1))  13.6 us
    ppermute x10, waiting for transfers between devices, direct_reduce_scatter(): total = total + lax.ppermute(take(x, (me + k) % n), axes, ring_pairs(n, k))  10.1 us
    ppermute x6, waiting for transfers between devices, rings_reduce_scatter(): got_b = lax.ppermute(acc_b, axes, ring_pairs(n, n - 1))  8.58 us
    add x1, other arithmetic, on_device(): grad = own_part + got  4.48 us
  transfers between devices with their start and end apart: 40, of which 18 were waited for; matrix products, arithmetic and copies ran while one was open for 1% of the time, Pallas kernels for 13%

commit v1 on v0

--- a/solution.py
+++ b/solution.py
@@ -221,10 +221,10 @@
         region_blocks, panel_y, tiles, rows_flat, live, me[None], partial_regions, True
     )
 
-    grad = own_part + got
-    grad = grad.reshape(n_y, n_zl, n_zh, n_x, jj, width)
-    part_a = grad[..., :hw]
-    part_b = grad[..., hw:].transpose(3, 0, 1, 2, 4, 5)
+    own_part = own_part.reshape(n_y, n_zl, n_zh, n_x, jj, width)
+    got = got.reshape(n_y, n_zl, n_zh, n_x, jj, width)
+    part_a = own_part[..., :hw] + got[..., :hw]
+    part_b = (own_part[..., hw:] + got[..., hw:]).transpose(3, 0, 1, 2, 4, 5)
     part_a, part_b = rings_reduce_scatter([(part_a, "y", n_y), (part_b, "x", n_x)])
     part_a = part_a.transpose(2, 0, 1, 3, 4)
     part_a, part_b = direct_reduce_scatter([(part_a, "x", n_x), (part_b, "y", n_y)])

time: 158 us -> 158 us (level)
    transpose x0 -> x1, other arithmetic: none -> 4.5 us  [on_device(): part_b = (own_part[..., hw:] + got[..., hw:]).transpose(3, 0, 1, 2, 4, 5)]
    add x1 -> x0, other arithmetic: 4.48 us -> none  [on_device(): grad = own_part + got]
  transfers between devices with their start and end apart: 40 -> 40, of which waited for: 18 -> 18; matrix products, arithmetic and copies ran while one was open for 1% -> 2% of each run, Pallas kernels for 13% -> 14%
where the time goes in v1:
time: 158 us; the launch traced here: 157 us
  starting transfers between devices  65.8 us (42%)
  Pallas kernels  41.2 us (26%)
  waiting for transfers between devices  40.5 us (26%)
  other arithmetic  6.19 us (4%)
  local copies, waits for them, and re-layouts  2.1 us (1%)
    pallas_call x2, Pallas kernels, local_grads(): pl.pallas_call(functools.partial(grad_kernel, first, last, ny), grid_spec...  41.2 us
    ppermute x16, starting transfers between devices, direct_all_gather(): buf = put(buf, lax.ppermute(x, axes, ring_pairs(n, k)), (me - k) % n)  29.3 us
    ppermute x10, starting transfers between devices, direct_reduce_scatter(): total = total + lax.ppermute(take(x, (me + k) % n), axes, ring_pairs(n, k))  20.5 us
    ppermute x16, waiting for transfers between devices, direct_all_gather(): buf = put(buf, lax.ppermute(x, axes, ring_pairs(n, k)), (me - k) % n)  14.5 us
    ppermute x6, starting transfers between devices, rings_reduce_scatter(): got_b = lax.ppermute(acc_b, axes, ring_pairs(n, n - 1))  13.4 us
    ppermute x10, waiting for transfers between devices, direct_reduce_scatter(): total = total + lax.ppermute(take(x, (me + k) % n), axes, ring_pairs(n, k))  10.1 us
    ppermute x6, waiting for transfers between devices, rings_reduce_scatter(): got_b = lax.ppermute(acc_b, axes, ring_pairs(n, n - 1))  8.42 us
    transpose x1, other arithmetic, on_device(): part_b = (own_part[..., hw:] + got[..., hw:]).transpose(3, 0, 1, 2, 4, 5)  4.5 us
  transfers between devices with their start and end apart: 40, of which 18 were waited for; matrix products, arithmetic and copies ran while one was open for 2% of the time, Pallas kernels for 14%

profile of v1, /device:TPU:32, one launch (start us, length us, event | category | flops | bytes accessed | tf_op | source)
XLA Modules:
  0.0 156.9 jit_solution(18235678342945033571)
XLA Ops:
  0.6 6.4 %collective-permute-start = (bf16[16,512]{1,0:T(8,128)(2,1)}, bf16[16,512]{1,0:T(8,128)(2,1)S(1)}, u32[]{:S(2)}, u32[]{:S(2)}) collective-permute-start(bf16[16,512]{1,0:T(8,128)(2,1)} %bitcast.164), channel_id=1, source_target_pairs={{0,128},{128,0},{1,129},{129,1},{2,130},{130,2},{3,131},{131,3},{4... | collective-permute-start | bytes 49160 | tf_op jit(solution)/shard_map/ppermute | solution.py:188
  8.9 1.6 collective-permute-start.1
  10.5 2.3 %collective-permute-start.2 = (bf16[2,16,512]{2,1,0:T(8,128)(2,1)S(1)}, bf16[2,16,512]{2,1,0:T(8,128)(2,1)S(1)}, u32[]{:S(2)}, u32[]{:S(2)}) collective-permute-start(bf16[2,16,512]{2,1,0:T(8,128)(2,1)S(1)} %bitcast_dynamic-update-slice_fusion.20), channel_id=1, source_target_pairs={{0,16},{8,24},{16,0},{24,8},{1,17},{9,25},{17,1},{25,9},{2,18},{10... | collective-permute-start | bytes 98312 | tf_op jit(solution)/shard_map/ppermute | solution.py:188
  17.8 2.7 %collective-permute-start.5 = (bf16[4,2,16,256]{3,2,1,0:T(8,128)(2,1)S(1)}, bf16[4,2,16,256]{3,2,1,0:T(8,128)(2,1)S(1)}, u32[]{:S(2)}, u32[]{:S(2)}) collective-permute-start(bf16[4,2,16,256]{3,2,1,0:T(8,128)(2,1)S(1)} %get-tuple-element.25), channel_id=1, source_target_pairs={{0,64},{32,96},{64,0},{96,32},{1,65},{33,97},{65,1},{97,33},{2,66}... | collective-permute-start | bytes 196616 | tf_op jit(solution)/shard_map/ppermute | solution.py:188
  20.5 1.4 collective-permute-start.6
  22.0 1.6 %collective-permute-start.10 = (bf16[4,2,16,256]{3,2,1,0:T(8,128)(2,1)S(1)}, bf16[4,2,16,256]{3,2,1,0:T(8,128)(2,1)S(1)}, u32[]{:S(2)}, u32[]{:S(2)}) collective-permute-start(bf16[4,2,16,256]{3,2,1,0:T(8,128)(2,1)S(1)} %get-tuple-element.26), channel_id=1, source_target_pairs={{0,2},{2,4},{4,6},{6,0},{1,3},{3,5},{5,7},{7,1},{8,10},{10,12},{12... | collective-permute-start | bytes 196616 | tf_op jit(solution)/shard_map/ppermute | solution.py:188
  23.6 2.9 %collective-permute-start.11 = (bf16[4,2,16,256]{3,2,1,0:T(8,128)(2,1)S(1)}, bf16[4,2,16,256]{3,2,1,0:T(8,128)(2,1)S(1)}, u32[]{:S(2)}, u32[]{:S(2)}) collective-permute-start(bf16[4,2,16,256]{3,2,1,0:T(8,128)(2,1)S(1)} %get-tuple-element.26), channel_id=1, source_target_pairs={{0,4},{2,6},{4,0},{6,2},{1,5},{3,7},{5,1},{7,3},{8,12},{10,14},{12... | collective-permute-start | bytes 196616 | tf_op jit(solution)/shard_map/ppermute | solution.py:188
  29.6 2.0 %collective-permute-start.9 = (bf16[4,4,2,16,256]{4,3,2,1,0:T(8,128)(2,1)S(1)}, bf16[4,4,2,16,256]{4,3,2,1,0:T(8,128)(2,1)S(1)}, u32[]{:S(2)}, u32[]{:S(2)}) collective-permute-start(bf16[4,4,2,16,256]{4,3,2,1,0:T(8,128)(2,1)S(1)} %bitcast_dynamic-update-slice_fusion.12), channel_id=1, source_target_pairs={{0,6},{2,0},{4,2},{6,4},{1,7},{3,1},{5,3},{7,5},{8,14},{10,8},{12,... | collective-permute-start | bytes 786440 | tf_op jit(solution)/shard_map/ppermute | solution.py:188
  32.4 2.6 %collective-permute-start.14 = (bf16[4,4,2,16,256]{4,3,2,1,0:T(8,128)(2,1)S(1)}, bf16[4,4,2,16,256]{4,3,2,1,0:T(8,128)(2,1)S(1)}, u32[]{:S(2)}, u32[]{:S(2)}) collective-permute-start(bf16[4,4,2,16,256]{4,3,2,1,0:T(8,128)(2,1)S(1)} %bitcast_dynamic-update-slice_fusion.8), channel_id=1, source_target_pairs={{0,64},{32,96},{64,0},{96,32},{1,65},{33,97},{65,1},{97,33},{2,66}... | collective-permute-start | bytes 786440 | tf_op jit(solution)/shard_map/ppermute | solution.py:188
  35.3 4.3 %collective-permute-done.7 = bf16[4,4,2,16,256]{4,3,2,1,0:T(8,128)(2,1)S(1)} collective-permute-done((bf16[4,4,2,16,256]{4,3,2,1,0:T(8,128)(2,1)S(1)}, bf16[4,4,2,16,256]{4,3,2,1,0:T(8,128)(2,1)S(1)}, u32[]{:S(2)}, u32[]{:S(2)}) %collective-permute-start.7) | collective-permute-done | bytes 262176 | tf_op jit(solution)/shard_map/ppermute | solution.py:188
  40.4 1.7 %collective-permute-done.14 = bf16[4,4,2,16,256]{4,3,2,1,0:T(8,128)(2,1)S(1)} collective-permute-done((bf16[4,4,2,16,256]{4,3,2,1,0:T(8,128)(2,1)S(1)}, bf16[4,4,2,16,256]{4,3,2,1,0:T(8,128)(2,1)S(1)}, u32[]{:S(2)}, u32[]{:S(2)}) %collective-permute-start.14) | collective-permute-done | bytes 262176 | tf_op jit(solution)/shard_map/ppermute | solution.py:188
  42.2 3.8 %collective-permute-done.15 = bf16[4,4,2,16,256]{4,3,2,1,0:T(8,128)(2,1)S(1)} collective-permute-done((bf16[4,4,2,16,256]{4,3,2,1,0:T(8,128)(2,1)S(1)}, bf16[4,4,2,16,256]{4,3,2,1,0:T(8,128)(2,1)S(1)}, u32[]{:S(2)}, u32[]{:S(2)}) %collective-permute-start.15) | collective-permute-done | bytes 262176 | tf_op jit(solution)/shard_map/ppermute | solution.py:188
  46.9 4.0 %collective-permute-done.16.v_ref = bf16[4,4,128,512]{3,2,1,0:T(8,128)(2,1)} collective-permute-done((bf16[4,4,128,512]{3,2,1,0:T(8,128)(2,1)S(1)}, bf16[4,4,128,512]{3,2,1,0:T(8,128)(2,1)}, u32[]{:S(2)}, u32[]{:S(2)}) %collective-permute-start.16) | collective-permute-done | bytes 2097184 | tf_op jit(solution)/shard_map/ppermute | solution.py:212
  50.9 20.0 %shard_map.68 = (f32[8,128,512]{2,1,0:T(8,128)}, f32[4,4,128,512]{3,2,1,0:T(8,128)}) custom-call(s32[192]{0:T(256)S(1)} %reshape_squeeze.3.rows_ref, s32[32]{0:T(128)S(1)} %bitcast.160, s32[1]{0:T(128)} %bitcast.36.sel_ref, bf16[8,128,512]{2,1,0:T(8,128)(2,1)S(1)} %bitcast.158, bf16[4,4,128,512]{3,2,1,0:T(8,128)(2,1)} %collective-permute-done.16.v_ref, ...), custom_call_target="tpu_custom_call" | custom-call | flops 4831838208 | bytes 14680064 | tf_op jit(solution)/shard_map/pallas_call | solution.py:100
  71.0 21.2 %shard_map.69 = (f32[8,128,512]{2,1,0:T(8,128)}, f32[4,4,128,512]{3,2,1,0:T(8,128)}) custom-call(s32[192]{0:T(256)S(1)} %reshape_squeeze.3.rows_ref, s32[32]{0:T(128)S(1)} %bitcast.161, s32[1]{0:T(128)} %bitcast.1.sel_ref, bf16[8,128,512]{2,1,0:T(8,128)(2,1)S(1)} %bitcast.159, ...), custom_call_target="tpu_custom_call", output_to_operand_aliasing={{0}: (7, {})} | custom-call | flops 4831838208 | bytes 14680064 | tf_op jit(solution)/shard_map/pallas_call | solution.py:100
  92.2 4.5 %fusion = (f32[4,4,4,2,16,256]{5,4,0,3,2,1:T(8,128)S(1)}, f32[4,4,2,4,16,256]{5,4,3,2,1,0:T(8,128)S(1)}) fusion(f32[4,4,2,4,16,512]{5,4,3,2,1,0:T(8,128)} %bitcast.39, f32[4,4,2,4,16,512]{5,4,3,2,1,0:T(8,128)} %bitcast.162), kind=kLoop, calls=%fused_computation.1 | loop fusion | flops 1048576 | bytes 12582912 | tf_op jit(solution)/shard_map/transpose | solution.py:227
  101.6 4.0 %collective-permute-done.30 = f32[2,4,2,16,256]{4,3,2,1,0:T(8,128)S(1)} collective-permute-done((f32[2,4,2,16,256]{4,3,2,1,0:T(8,128)S(1)}, f32[2,4,2,16,256]{4,3,2,1,0:T(8,128)S(1)}, u32[]{:S(2)}, u32[]{:S(2)}) %collective-permute-start.30) | collective-permute-done | bytes 262176 | tf_op jit(solution)/shard_map/ppermute | solution.py:143
  105.6 2.5 %collective-permute-start.31 = (f32[2,4,2,16,256]{4,3,2,1,0:T(8,128)S(1)}, f32[2,4,2,16,256]{4,3,2,1,0:T(8,128)S(1)}, u32[]{:S(2)}, u32[]{:S(2)}) collective-permute-start(f32[2,4,2,16,256]{4,3,2,1,0:T(8,128)S(1)} %bitcast_add_fusion.2), channel_id=1, source_target_pairs={{0,96},{32,0},{64,32},{96,64},{1,97},{33,1},{65,33},{97,65},{2,98}... | collective-permute-start | bytes 786440 | tf_op jit(solution)/shard_map/ppermute | solution.py:143
  108.3 2.2 %collective-permute-start.22 = (f32[2,2,4,16,256]{4,3,2,1,0:T(8,128)S(1)}, f32[2,2,4,16,256]{4,3,2,1,0:T(8,128)S(1)}, u32[]{:S(2)}, u32[]{:S(2)}) collective-permute-start(f32[2,2,4,16,256]{4,3,2,1,0:T(8,128)S(1)} %bitcast_add_fusion.8), channel_id=1, source_target_pairs={{0,6},{2,0},{4,2},{6,4},{1,7},{3,1},{5,3},{7,5},{8,14},{10,8},{12,... | collective-permute-start | bytes 786440 | tf_op jit(solution)/shard_map/ppermute | solution.py:143
  110.9 2.6 %collective-permute-done.31 = f32[2,4,2,16,256]{4,3,2,1,0:T(8,128)S(1)} collective-permute-done((f32[2,4,2,16,256]{4,3,2,1,0:T(8,128)S(1)}, f32[2,4,2,16,256]{4,3,2,1,0:T(8,128)S(1)}, u32[]{:S(2)}, u32[]{:S(2)}) %collective-permute-start.31) | collective-permute-done | bytes 262176 | tf_op jit(solution)/shard_map/ppermute | solution.py:143
  113.5 3.7 %collective-permute-start.32 = (f32[2,4,2,16,256]{4,3,2,1,0:T(8,128)S(1)}, f32[2,4,2,16,256]{4,3,2,1,0:T(8,128)S(1)}, u32[]{:S(2)}, u32[]{:S(2)}) collective-permute-start(f32[2,4,2,16,256]{4,3,2,1,0:T(8,128)S(1)} %bitcast_add_fusion.1), channel_id=1, source_target_pairs={{0,96},{32,0},{64,32},{96,64},{1,97},{33,1},{65,33},{97,65},{2,98}... | collective-permute-start | bytes 786440 | tf_op jit(solution)/shard_map/ppermute | solution.py:143
  117.4 2.2 %collective-permute-start.23 = (f32[2,2,4,16,256]{4,3,2,1,0:T(8,128)S(1)}, f32[2,2,4,16,256]{4,3,2,1,0:T(8,128)S(1)}, u32[]{:S(2)}, u32[]{:S(2)}) collective-permute-start(f32[2,2,4,16,256]{4,3,2,1,0:T(8,128)S(1)} %bitcast_add_fusion.7), channel_id=1, source_target_pairs={{0,6},{2,0},{4,2},{6,4},{1,7},{3,1},{5,3},{7,5},{8,14},{10,8},{12,... | collective-permute-start | bytes 786440 | tf_op jit(solution)/shard_map/ppermute | solution.py:143
  119.8 1.8 %collective-permute-done.32 = f32[2,4,2,16,256]{4,3,2,1,0:T(8,128)S(1)} collective-permute-done((f32[2,4,2,16,256]{4,3,2,1,0:T(8,128)S(1)}, f32[2,4,2,16,256]{4,3,2,1,0:T(8,128)S(1)}, u32[]{:S(2)}, u32[]{:S(2)}) %collective-permute-start.32) | collective-permute-done | bytes 262176 | tf_op jit(solution)/shard_map/ppermute | solution.py:143
  121.6 3.5 %collective-permute-done.29 = f32[2,4,2,16,256]{4,3,2,1,0:T(8,128)S(1)} collective-permute-done((f32[2,4,2,16,256]{4,3,2,1,0:T(8,128)S(1)}, f32[2,4,2,16,256]{4,3,2,1,0:T(8,128)S(1)}, u32[]{:S(2)}, u32[]{:S(2)}) %collective-permute-start.29) | collective-permute-done | bytes 262176 | tf_op jit(solution)/shard_map/ppermute | solution.py:142
  125.7 3.3 %collective-permute-start.34 = (f32[4,2,16,256]{3,2,1,0:T(8,128)S(1)}, f32[4,2,16,256]{3,2,1,0:T(8,128)S(1)}, u32[]{:S(2)}, u32[]{:S(2)}) collective-permute-start(f32[4,2,16,256]{3,2,1,0:T(8,128)S(1)} %get-tuple-element.17), channel_id=1, source_target_pairs={{0,4},{2,6},{4,0},{6,2},{1,5},{3,7},{5,1},{7,3},{8,12},{10,14},{12... | collective-permute-start | bytes 393224 | tf_op jit(solution)/shard_map/ppermute | solution.py:177
  129.5 5.2 %collective-permute-start.25 = (f32[4,2,16,256]{3,2,1,0:T(8,128)S(1)}, f32[4,2,16,256]{3,2,1,0:T(8,128)S(1)}, u32[]{:S(2)}, u32[]{:S(2)}) collective-permute-start(f32[4,2,16,256]{3,2,1,0:T(8,128)S(1)} %get-tuple-element.20), channel_id=1, source_target_pairs={{0,64},{32,96},{64,0},{96,32},{1,65},{33,97},{65,1},{97,33},{2,66}... | collective-permute-start | bytes 393224 | tf_op jit(solution)/shard_map/ppermute | solution.py:177
  136.1 2.9 %collective-permute-done.25 = f32[4,2,16,256]{3,2,1,0:T(8,128)S(1)} collective-permute-done((f32[4,2,16,256]{3,2,1,0:T(8,128)S(1)}, f32[4,2,16,256]{3,2,1,0:T(8,128)S(1)}, u32[]{:S(2)}, u32[]{:S(2)}) %collective-permute-start.25) | collective-permute-done | bytes 131104 | tf_op jit(solution)/shard_map/ppermute | solution.py:177
  140.8 2.9 %collective-permute-start.37 = (f32[2,16,512]{2,1,0:T(8,128)S(1)}, f32[2,16,512]{2,1,0:T(8,128)S(1)}, u32[]{:S(2)}, u32[]{:S(2)}) collective-permute-start(f32[2,16,512]{2,1,0:T(8,128)S(1)} %get-tuple-element.23), channel_id=1, source_target_pairs={{0,16},{8,24},{16,0},{24,8},{1,17},{9,25},{17,1},{25,9},{2,18},{10... | collective-permute-start | bytes 196616 | tf_op jit(solution)/shard_map/ppermute | solution.py:177
  144.7 2.0 %collective-permute-done.37 = f32[2,16,512]{2,1,0:T(8,128)S(1)} collective-permute-done((f32[2,16,512]{2,1,0:T(8,128)S(1)}, f32[2,16,512]{2,1,0:T(8,128)S(1)}, u32[]{:S(2)}, u32[]{:S(2)}) %collective-permute-start.37) | collective-permute-done | bytes 65568 | tf_op jit(solution)/shard_map/ppermute | solution.py:177
  146.8 1.6 %collective-permute-done.38 = f32[2,16,512]{2,1,0:T(8,128)S(1)} collective-permute-done((f32[2,16,512]{2,1,0:T(8,128)S(1)}, f32[2,16,512]{2,1,0:T(8,128)S(1)}, u32[]{:S(2)}, u32[]{:S(2)}) %collective-permute-start.38) | collective-permute-done | bytes 65568 | tf_op jit(solution)/shard_map/ppermute | solution.py:177
  148.4 5.2 %collective-permute-start.39 = (f32[16,512]{1,0:T(8,128)S(1)}, f32[16,512]{1,0:T(8,128)S(1)}, u32[]{:S(2)}, u32[]{:S(2)}) collective-permute-start(f32[16,512]{1,0:T(8,128)S(1)} %dynamic-slice_bitcast_fusion.4), channel_id=1, source_target_pairs={{0,128},{128,0},{1,129},{129,1},{2,130},{130,2},{3,131},{131,3},{4... | collective-permute-start | bytes 98312 | tf_op jit(solution)/shard_map/ppermute | solution.py:177
  153.5 2.8 %collective-permute-done.39 = f32[16,512]{1,0:T(8,128)S(1)} collective-permute-done((f32[16,512]{1,0:T(8,128)S(1)}, f32[16,512]{1,0:T(8,128)S(1)}, u32[]{:S(2)}, u32[]{:S(2)}) %collective-permute-start.39) | collective-permute-done | bytes 32800 | tf_op jit(solution)/shard_map/ppermute | solution.py:177
  (117 shorter events, 24.6 us)
Async XLA Ops:
  0.6 8.3 %collective-permute-start = (bf16[16,512]{1,0:T(8,128)(2,1)}, bf16[16,512]{1,0:T(8,128)(2,1)S(1)}, u32[]{:S(2)}, u32[]{:S(2)}) collective-permute-start(bf16[16,512]{1,0:T(8,128)(2,1)} %bitcast.164), channel_id=1, source_target_pairs={{0,128},{128,0},{1,129},{129,1},{2,130},{130,2},{3,131},{131,3},{4... | collective-permute-start | bytes 49160 | tf_op jit(solution)/shard_map/ppermute | solution.py:188
  16.7 9.8 %collective-permute-start.4 = (bf16[4,2,16,256]{3,2,1,0:T(8,128)(2,1)S(1)}, bf16[4,2,16,256]{3,2,1,0:T(8,128)(2,1)S(1)}, u32[]{:S(2)}, u32[]{:S(2)}) collective-permute-start(bf16[4,2,16,256]{3,2,1,0:T(8,128)(2,1)S(1)} %get-tuple-element.25), channel_id=1, source_target_pairs={{0,32},{32,64},{64,96},{96,0},{1,33},{33,65},{65,97},{97,1},{2,34}... | collective-permute-start | bytes 196616 | tf_op jit(solution)/shard_map/ppermute | solution.py:188
  17.8 10.2 %collective-permute-start.5 = (bf16[4,2,16,256]{3,2,1,0:T(8,128)(2,1)S(1)}, bf16[4,2,16,256]{3,2,1,0:T(8,128)(2,1)S(1)}, u32[]{:S(2)}, u32[]{:S(2)}) collective-permute-start(bf16[4,2,16,256]{3,2,1,0:T(8,128)(2,1)S(1)} %get-tuple-element.25), channel_id=1, source_target_pairs={{0,64},{32,96},{64,0},{96,32},{1,65},{33,97},{65,1},{97,33},{2,66}... | collective-permute-start | bytes 196616 | tf_op jit(solution)/shard_map/ppermute | solution.py:188
  20.5 7.5 %collective-permute-start.6 = (bf16[4,2,16,256]{3,2,1,0:T(8,128)(2,1)S(1)}, bf16[4,2,16,256]{3,2,1,0:T(8,128)(2,1)S(1)}, u32[]{:S(2)}, u32[]{:S(2)}) collective-permute-start(bf16[4,2,16,256]{3,2,1,0:T(8,128)(2,1)S(1)} %get-tuple-element.25), channel_id=1, source_target_pairs={{0,96},{32,0},{64,32},{96,64},{1,97},{33,1},{65,33},{97,65},{2,98}... | collective-permute-start | bytes 196616 | tf_op jit(solution)/shard_map/ppermute | solution.py:188
  22.0 7.6 %collective-permute-start.10 = (bf16[4,2,16,256]{3,2,1,0:T(8,128)(2,1)S(1)}, bf16[4,2,16,256]{3,2,1,0:T(8,128)(2,1)S(1)}, u32[]{:S(2)}, u32[]{:S(2)}) collective-permute-start(bf16[4,2,16,256]{3,2,1,0:T(8,128)(2,1)S(1)} %get-tuple-element.26), channel_id=1, source_target_pairs={{0,2},{2,4},{4,6},{6,0},{1,3},{3,5},{5,7},{7,1},{8,10},{10,12},{12... | collective-permute-start | bytes 196616 | tf_op jit(solution)/shard_map/ppermute | solution.py:188
  23.6 8.0 %collective-permute-start.11 = (bf16[4,2,16,256]{3,2,1,0:T(8,128)(2,1)S(1)}, bf16[4,2,16,256]{3,2,1,0:T(8,128)(2,1)S(1)}, u32[]{:S(2)}, u32[]{:S(2)}) collective-permute-start(bf16[4,2,16,256]{3,2,1,0:T(8,128)(2,1)S(1)} %get-tuple-element.26), channel_id=1, source_target_pairs={{0,4},{2,6},{4,0},{6,2},{1,5},{3,7},{5,1},{7,3},{8,12},{10,14},{12... | collective-permute-start | bytes 196616 | tf_op jit(solution)/shard_map/ppermute | solution.py:188
  28.1 11.5 %collective-permute-start.7 = (bf16[4,4,2,16,256]{4,3,2,1,0:T(8,128)(2,1)S(1)}, bf16[4,4,2,16,256]{4,3,2,1,0:T(8,128)(2,1)S(1)}, u32[]{:S(2)}, u32[]{:S(2)}) collective-permute-start(bf16[4,4,2,16,256]{4,3,2,1,0:T(8,128)(2,1)S(1)} %bitcast_dynamic-update-slice_fusion.12), channel_id=1, source_target_pairs={{0,2},{2,4},{4,6},{6,0},{1,3},{3,5},{5,7},{7,1},{8,10},{10,12},{12... | collective-permute-start | bytes 786440 | tf_op jit(solution)/shard_map/ppermute | solution.py:188
  28.8 10.8 %collective-permute-start.8 = (bf16[4,4,2,16,256]{4,3,2,1,0:T(8,128)(2,1)S(1)}, bf16[4,4,2,16,256]{4,3,2,1,0:T(8,128)(2,1)S(1)}, u32[]{:S(2)}, u32[]{:S(2)}) collective-permute-start(bf16[4,4,2,16,256]{4,3,2,1,0:T(8,128)(2,1)S(1)} %bitcast_dynamic-update-slice_fusion.12), channel_id=1, source_target_pairs={{0,4},{2,6},{4,0},{6,2},{1,5},{3,7},{5,1},{7,3},{8,12},{10,14},{12... | collective-permute-start | bytes 786440 | tf_op jit(solution)/shard_map/ppermute | solution.py:188
  29.6 10.7 %collective-permute-start.9 = (bf16[4,4,2,16,256]{4,3,2,1,0:T(8,128)(2,1)S(1)}, bf16[4,4,2,16,256]{4,3,2,1,0:T(8,128)(2,1)S(1)}, u32[]{:S(2)}, u32[]{:S(2)}) collective-permute-start(bf16[4,4,2,16,256]{4,3,2,1,0:T(8,128)(2,1)S(1)} %bitcast_dynamic-update-slice_fusion.12), channel_id=1, source_target_pairs={{0,6},{2,0},{4,2},{6,4},{1,7},{3,1},{5,3},{7,5},{8,14},{10,8},{12,... | collective-permute-start | bytes 786440 | tf_op jit(solution)/shard_map/ppermute | solution.py:188
  31.7 8.7 %collective-permute-start.13 = (bf16[4,4,2,16,256]{4,3,2,1,0:T(8,128)(2,1)S(1)}, bf16[4,4,2,16,256]{4,3,2,1,0:T(8,128)(2,1)S(1)}, u32[]{:S(2)}, u32[]{:S(2)}) collective-permute-start(bf16[4,4,2,16,256]{4,3,2,1,0:T(8,128)(2,1)S(1)} %bitcast_dynamic-update-slice_fusion.8), channel_id=1, source_target_pairs={{0,32},{32,64},{64,96},{96,0},{1,33},{33,65},{65,97},{97,1},{2,34}... | collective-permute-start | bytes 786440 | tf_op jit(solution)/shard_map/ppermute | solution.py:188
  32.4 9.8 %collective-permute-start.14 = (bf16[4,4,2,16,256]{4,3,2,1,0:T(8,128)(2,1)S(1)}, bf16[4,4,2,16,256]{4,3,2,1,0:T(8,128)(2,1)S(1)}, u32[]{:S(2)}, u32[]{:S(2)}) collective-permute-start(bf16[4,4,2,16,256]{4,3,2,1,0:T(8,128)(2,1)S(1)} %bitcast_dynamic-update-slice_fusion.8), channel_id=1, source_target_pairs={{0,64},{32,96},{64,0},{96,32},{1,65},{33,97},{65,1},{97,33},{2,66}... | collective-permute-start | bytes 786440 | tf_op jit(solution)/shard_map/ppermute | solution.py:188
  39.6 6.4 %collective-permute-start.15 = (bf16[4,4,2,16,256]{4,3,2,1,0:T(8,128)(2,1)S(1)}, bf16[4,4,2,16,256]{4,3,2,1,0:T(8,128)(2,1)S(1)}, u32[]{:S(2)}, u32[]{:S(2)}) collective-permute-start(bf16[4,4,2,16,256]{4,3,2,1,0:T(8,128)(2,1)S(1)} %bitcast_dynamic-update-slice_fusion.8), channel_id=1, source_target_pairs={{0,96},{32,0},{64,32},{96,64},{1,97},{33,1},{65,33},{97,65},{2,98}... | collective-permute-start | bytes 786440 | tf_op jit(solution)/shard_map/ppermute | solution.py:188
  70.8 21.4 %collective-permute-start.17 = (f32[4,4,128,512]{3,2,1,0:T(8,128)}, f32[4,4,128,512]{3,2,1,0:T(8,128)}, u32[]{:S(2)}, u32[]{:S(2)}) collective-permute-start(f32[4,4,128,512]{3,2,1,0:T(8,128)} %get-tuple-element.9), channel_id=1, source_target_pairs={{0,1},{1,0},{2,3},{3,2},{4,5},{5,4},{6,7},{7,6},{8,9},{9,8},{10,11... | collective-permute-start | bytes 12582920 | tf_op jit(solution)/shard_map/ppermute | solution.py:219
  96.9 8.7 %collective-permute-start.30 = (f32[2,4,2,16,256]{4,3,2,1,0:T(8,128)S(1)}, f32[2,4,2,16,256]{4,3,2,1,0:T(8,128)S(1)}, u32[]{:S(2)}, u32[]{:S(2)}) collective-permute-start(f32[2,4,2,16,256]{4,3,2,1,0:T(8,128)S(1)} %dynamic-slice_bitcast_fusion), channel_id=1, source_target_pairs={{0,96},{32,0},{64,32},{96,64},{1,97},{33,1},{65,33},{97,65},{2,98}... | collective-permute-start | bytes 786440 | tf_op jit(solution)/shard_map/ppermute | solution.py:143
  98.2 9.9 %collective-permute-start.27 = (f32[2,4,2,16,256]{4,3,2,1,0:T(8,128)S(1)}, f32[2,4,2,16,256]{4,3,2,1,0:T(8,128)S(1)}, u32[]{:S(2)}, u32[]{:S(2)}) collective-permute-start(f32[2,4,2,16,256]{4,3,2,1,0:T(8,128)S(1)} %dynamic-slice_bitcast_fusion.1), channel_id=1, source_target_pairs={{0,32},{32,64},{64,96},{96,0},{1,33},{33,65},{65,97},{97,1},{2,34}... | collective-permute-start | bytes 786440 | tf_op jit(solution)/shard_map/ppermute | solution.py:142
  99.4 8.9 %collective-permute-start.21 = (f32[2,2,4,16,256]{4,3,2,1,0:T(8,128)S(1)}, f32[2,2,4,16,256]{4,3,2,1,0:T(8,128)S(1)}, u32[]{:S(2)}, u32[]{:S(2)}) collective-permute-start(f32[2,2,4,16,256]{4,3,2,1,0:T(8,128)S(1)} %dynamic-slice_bitcast_fusion.2), channel_id=1, source_target_pairs={{0,6},{2,0},{4,2},{6,4},{1,7},{3,1},{5,3},{7,5},{8,14},{10,8},{12,... | collective-permute-start | bytes 786440 | tf_op jit(solution)/shard_map/ppermute | solution.py:143
  100.8 9.7 %collective-permute-start.18 = (f32[2,2,4,16,256]{4,3,2,1,0:T(8,128)S(1)}, f32[2,2,4,16,256]{4,3,2,1,0:T(8,128)S(1)}, u32[]{:S(2)}, u32[]{:S(2)}) collective-permute-start(f32[2,2,4,16,256]{4,3,2,1,0:T(8,128)S(1)} %dynamic-slice_bitcast_fusion.3), channel_id=1, source_target_pairs={{0,2},{2,4},{4,6},{6,0},{1,3},{3,5},{5,7},{7,1},{8,10},{10,12},{12... | collective-permute-start | bytes 786440 | tf_op jit(solution)/shard_map/ppermute | solution.py:142
  105.6 7.8 %collective-permute-start.31 = (f32[2,4,2,16,256]{4,3,2,1,0:T(8,128)S(1)}, f32[2,4,2,16,256]{4,3,2,1,0:T(8,128)S(1)}, u32[]{:S(2)}, u32[]{:S(2)}) collective-permute-start(f32[2,4,2,16,256]{4,3,2,1,0:T(8,128)S(1)} %bitcast_add_fusion.2), channel_id=1, source_target_pairs={{0,96},{32,0},{64,32},{96,64},{1,97},{33,1},{65,33},{97,65},{2,98}... | collective-permute-start | bytes 786440 | tf_op jit(solution)/shard_map/ppermute | solution.py:143
  108.2 9.1 %collective-permute-start.28 = (f32[2,4,2,16,256]{4,3,2,1,0:T(8,128)S(1)}, f32[2,4,2,16,256]{4,3,2,1,0:T(8,128)S(1)}, u32[]{:S(2)}, u32[]{:S(2)}) collective-permute-start(f32[2,4,2,16,256]{4,3,2,1,0:T(8,128)S(1)} %bitcast_add_fusion.5), channel_id=1, source_target_pairs={{0,32},{32,64},{64,96},{96,0},{1,33},{33,65},{65,97},{97,1},{2,34}... | collective-permute-start | bytes 786440 | tf_op jit(solution)/shard_map/ppermute | solution.py:142
  108.3 9.0 %collective-permute-start.22 = (f32[2,2,4,16,256]{4,3,2,1,0:T(8,128)S(1)}, f32[2,2,4,16,256]{4,3,2,1,0:T(8,128)S(1)}, u32[]{:S(2)}, u32[]{:S(2)}) collective-permute-start(f32[2,2,4,16,256]{4,3,2,1,0:T(8,128)S(1)} %bitcast_add_fusion.8), channel_id=1, source_target_pairs={{0,6},{2,0},{4,2},{6,4},{1,7},{3,1},{5,3},{7,5},{8,14},{10,8},{12,... | collective-permute-start | bytes 786440 | tf_op jit(solution)/shard_map/ppermute | solution.py:143
  110.6 9.1 %collective-permute-start.19 = (f32[2,2,4,16,256]{4,3,2,1,0:T(8,128)S(1)}, f32[2,2,4,16,256]{4,3,2,1,0:T(8,128)S(1)}, u32[]{:S(2)}, u32[]{:S(2)}) collective-permute-start(f32[2,2,4,16,256]{4,3,2,1,0:T(8,128)S(1)} %bitcast_add_fusion.11), channel_id=1, source_target_pairs={{0,2},{2,4},{4,6},{6,0},{1,3},{3,5},{5,7},{7,1},{8,10},{10,12},{12... | collective-permute-start | bytes 786440 | tf_op jit(solution)/shard_map/ppermute | solution.py:142
  113.5 8.1 %collective-permute-start.32 = (f32[2,4,2,16,256]{4,3,2,1,0:T(8,128)S(1)}, f32[2,4,2,16,256]{4,3,2,1,0:T(8,128)S(1)}, u32[]{:S(2)}, u32[]{:S(2)}) collective-permute-start(f32[2,4,2,16,256]{4,3,2,1,0:T(8,128)S(1)} %bitcast_add_fusion.1), channel_id=1, source_target_pairs={{0,96},{32,0},{64,32},{96,64},{1,97},{33,1},{65,33},{97,65},{2,98}... | collective-permute-start | bytes 786440 | tf_op jit(solution)/shard_map/ppermute | solution.py:143
  117.3 7.9 %collective-permute-start.29 = (f32[2,4,2,16,256]{4,3,2,1,0:T(8,128)S(1)}, f32[2,4,2,16,256]{4,3,2,1,0:T(8,128)S(1)}, u32[]{:S(2)}, u32[]{:S(2)}) collective-permute-start(f32[2,4,2,16,256]{4,3,2,1,0:T(8,128)S(1)} %bitcast_add_fusion.4), channel_id=1, source_target_pairs={{0,32},{32,64},{64,96},{96,0},{1,33},{33,65},{65,97},{97,1},{2,34}... | collective-permute-start | bytes 786440 | tf_op jit(solution)/shard_map/ppermute | solution.py:142
  117.4 11.8 %collective-permute-start.23 = (f32[2,2,4,16,256]{4,3,2,1,0:T(8,128)S(1)}, f32[2,2,4,16,256]{4,3,2,1,0:T(8,128)S(1)}, u32[]{:S(2)}, u32[]{:S(2)}) collective-permute-start(f32[2,2,4,16,256]{4,3,2,1,0:T(8,128)S(1)} %bitcast_add_fusion.7), channel_id=1, source_target_pairs={{0,6},{2,0},{4,2},{6,4},{1,7},{3,1},{5,3},{7,5},{8,14},{10,8},{12,... | collective-permute-start | bytes 786440 | tf_op jit(solution)/shard_map/ppermute | solution.py:143
  119.7 9.6 %collective-permute-start.20 = (f32[2,2,4,16,256]{4,3,2,1,0:T(8,128)S(1)}, f32[2,2,4,16,256]{4,3,2,1,0:T(8,128)S(1)}, u32[]{:S(2)}, u32[]{:S(2)}) collective-permute-start(f32[2,2,4,16,256]{4,3,2,1,0:T(8,128)S(1)} %bitcast_add_fusion.10), channel_id=1, source_target_pairs={{0,2},{2,4},{4,6},{6,0},{1,3},{3,5},{5,7},{7,1},{8,10},{10,12},{12... | collective-permute-start | bytes 786440 | tf_op jit(solution)/shard_map/ppermute | solution.py:142
  125.3 9.4 %collective-permute-start.33 = (f32[4,2,16,256]{3,2,1,0:T(8,128)S(1)}, f32[4,2,16,256]{3,2,1,0:T(8,128)S(1)}, u32[]{:S(2)}, u32[]{:S(2)}) collective-permute-start(f32[4,2,16,256]{3,2,1,0:T(8,128)S(1)} %get-tuple-element.16), channel_id=1, source_target_pairs={{0,2},{2,4},{4,6},{6,0},{1,3},{3,5},{5,7},{7,1},{8,10},{10,12},{12... | collective-permute-start | bytes 393224 | tf_op jit(solution)/shard_map/ppermute | solution.py:177
  125.7 10.1 %collective-permute-start.34 = (f32[4,2,16,256]{3,2,1,0:T(8,128)S(1)}, f32[4,2,16,256]{3,2,1,0:T(8,128)S(1)}, u32[]{:S(2)}, u32[]{:S(2)}) collective-permute-start(f32[4,2,16,256]{3,2,1,0:T(8,128)S(1)} %get-tuple-element.17), channel_id=1, source_target_pairs={{0,4},{2,6},{4,0},{6,2},{1,5},{3,7},{5,1},{7,3},{8,12},{10,14},{12... | collective-permute-start | bytes 393224 | tf_op jit(solution)/shard_map/ppermute | solution.py:177
  129.0 6.9 %collective-permute-start.35 = (f32[4,2,16,256]{3,2,1,0:T(8,128)S(1)}, f32[4,2,16,256]{3,2,1,0:T(8,128)S(1)}, u32[]{:S(2)}, u32[]{:S(2)}) collective-permute-start(f32[4,2,16,256]{3,2,1,0:T(8,128)S(1)} %get-tuple-element.18), channel_id=1, source_target_pairs={{0,6},{2,0},{4,2},{6,4},{1,7},{3,1},{5,3},{7,5},{8,14},{10,8},{12,... | collective-permute-start | bytes 393224 | tf_op jit(solution)/shard_map/ppermute | solution.py:177
  129.4 6.8 %collective-permute-start.24 = (f32[4,2,16,256]{3,2,1,0:T(8,128)S(1)}, f32[4,2,16,256]{3,2,1,0:T(8,128)S(1)}, u32[]{:S(2)}, u32[]{:S(2)}) collective-permute-start(f32[4,2,16,256]{3,2,1,0:T(8,128)S(1)} %get-tuple-element.19), channel_id=1, source_target_pairs={{0,32},{32,64},{64,96},{96,0},{1,33},{33,65},{65,97},{97,1},{2,34}... | collective-permute-start | bytes 393224 | tf_op jit(solution)/shard_map/ppermute | solution.py:177
  129.5 9.5 %collective-permute-start.25 = (f32[4,2,16,256]{3,2,1,0:T(8,128)S(1)}, f32[4,2,16,256]{3,2,1,0:T(8,128)S(1)}, u32[]{:S(2)}, u32[]{:S(2)}) collective-permute-start(f32[4,2,16,256]{3,2,1,0:T(8,128)S(1)} %get-tuple-element.20), channel_id=1, source_target_pairs={{0,64},{32,96},{64,0},{96,32},{1,65},{33,97},{65,1},{97,33},{2,66}... | collective-permute-start | bytes 393224 | tf_op jit(solution)/shard_map/ppermute | solution.py:177
  140.8 5.9 %collective-permute-start.37 = (f32[2,16,512]{2,1,0:T(8,128)S(1)}, f32[2,16,512]{2,1,0:T(8,128)S(1)}, u32[]{:S(2)}, u32[]{:S(2)}) collective-permute-start(f32[2,16,512]{2,1,0:T(8,128)S(1)} %get-tuple-element.23), channel_id=1, source_target_pairs={{0,16},{8,24},{16,0},{24,8},{1,17},{9,25},{17,1},{25,9},{2,18},{10... | collective-permute-start | bytes 196616 | tf_op jit(solution)/shard_map/ppermute | solution.py:177
  148.4 7.9 %collective-permute-start.39 = (f32[16,512]{1,0:T(8,128)S(1)}, f32[16,512]{1,0:T(8,128)S(1)}, u32[]{:S(2)}, u32[]{:S(2)}) collective-permute-start(f32[16,512]{1,0:T(8,128)S(1)} %dynamic-slice_bitcast_fusion.4), channel_id=1, source_target_pairs={{0,128},{128,0},{1,129},{129,1},{2,130},{130,2},{3,131},{131,3},{4... | collective-permute-start | bytes 98312 | tf_op jit(solution)/shard_map/ppermute | solution.py:177
  (12 other events, 75.3 us)

commit v2 on v1

--- a/solution.py
+++ b/solution.py
@@ -225,7 +225,7 @@
     got = got.reshape(n_y, n_zl, n_zh, n_x, jj, width)
     part_a = own_part[..., :hw] + got[..., :hw]
     part_b = (own_part[..., hw:] + got[..., hw:]).transpose(3, 0, 1, 2, 4, 5)
-    part_a, part_b = rings_reduce_scatter([(part_a, "y", n_y), (part_b, "x", n_x)])
+    part_a, part_b = direct_reduce_scatter([(part_a, "y", n_y), (part_b, "x", n_x)])
     part_a = part_a.transpose(2, 0, 1, 3, 4)
     part_a, part_b = direct_reduce_scatter([(part_a, "x", n_x), (part_b, "y", n_y)])
     grad = jnp.concatenate([part_a, part_b], axis=-1)

time: 158 us -> 166 us (1.051)
  waiting for transfers between devices: 40.5 us -> 55.5 us
  starting transfers between devices: 65.8 us -> 53.6 us
  local copies, waits for them, and re-layouts: 2.1 us -> 5.22 us
  other arithmetic: 6.19 us -> 8.83 us
    ppermute x10 -> x16, waiting for transfers between devices: 10.1 us -> 37.1 us  [direct_reduce_scatter(): total = total + lax.ppermute(take(x, (me + k) % n), axes, ring_pairs(n, k))]
    ppermute x12 -> x0, starting transfers between devices: 15.6 us -> none  [the longest x6 13.4 us: rings_reduce_scatter(): got_b = lax.ppermute(acc_b, axes, ring_pairs(n, n - 1))]
    ppermute x12 -> x0, waiting for transfers between devices: 11.9 us -> none  [the longest x6 8.42 us: rings_reduce_scatter(): got_b = lax.ppermute(acc_b, axes, ring_pairs(n, n - 1))]
    transpose x1 -> x0, other arithmetic: 4.5 us -> none  [on_device(): part_b = (own_part[..., hw:] + got[..., hw:]).transpose(3, 0, 1, 2, 4, 5)]
    add x12 -> x1, other arithmetic: 0.53 us -> 4.51 us  [on_device(): part_b = (own_part[..., hw:] + got[..., hw:]).transpose(3, 0, 1, 2, 4, 5)]
    ppermute x10 -> x16, starting transfers between devices: 20.5 us -> 23.9 us  [direct_reduce_scatter(): total = total + lax.ppermute(take(x, (me + k) % n), axes, ring_pairs(n, k))]
    add x3 -> x5, other arithmetic: 0.11 us -> 3.4 us  [direct_reduce_scatter(): total = total + lax.ppermute(take(x, (me + k) % n), axes, ring_pairs(n, k))]
    squeeze x5, local copies, waits for them, and re-layouts: 0.1 us -> 2.23 us  [take(): return lax.dynamic_index_in_dim(arr, index, 0, keepdims=False)]
  transfers between devices with their start and end apart: 40 -> 34, of which waited for: 18 -> 16; matrix products, arithmetic and copies ran while one was open for 2% -> 4% of each run, Pallas kernels for 14% -> 13%
where the time goes in v2:
time: 166 us; the launch traced here: 165 us
  waiting for transfers between devices  55.5 us (33%)
  starting transfers between devices  53.6 us (32%)
  Pallas kernels  40.7 us (25%)
  other arithmetic  8.83 us (5%)
  local copies, waits for them, and re-layouts  5.22 us (3%)
    pallas_call x2, Pallas kernels, local_grads(): pl.pallas_call(functools.partial(grad_kernel, first, last, ny), grid_spec...  40.7 us
    ppermute x16, waiting for transfers between devices, direct_reduce_scatter(): total = total + lax.ppermute(take(x, (me + k) % n), axes, ring_pairs(n, k))  37.1 us
    ppermute x16, starting transfers between devices, direct_all_gather(): buf = put(buf, lax.ppermute(x, axes, ring_pairs(n, k)), (me - k) % n)  29.3 us
    ppermute x16, starting transfers between devices, direct_reduce_scatter(): total = total + lax.ppermute(take(x, (me + k) % n), axes, ring_pairs(n, k))  23.9 us
    ppermute x16, waiting for transfers between devices, direct_all_gather(): buf = put(buf, lax.ppermute(x, axes, ring_pairs(n, k)), (me - k) % n)  14.5 us
    add x1, other arithmetic, on_device(): part_b = (own_part[..., hw:] + got[..., hw:]).transpose(3, 0, 1, 2, 4, 5)  4.51 us
    ppermute x1, waiting for transfers between devices, on_device(): panel_other = lax.ppermute(panel_y, 'core', swap)  3.99 us
    add x5, other arithmetic, direct_reduce_scatter(): total = total + lax.ppermute(take(x, (me + k) % n), axes, ring_pairs(n, k))  3.4 us
  transfers between devices with their start and end apart: 34, of which 16 were waited for; matrix products, arithmetic and copies ran while one was open for 4% of the time, Pallas kernels for 13%

profile of v2, /device:TPU:32, one launch (start us, length us, event | category | flops | bytes accessed | tf_op | source)
XLA Modules:
  0.0 165.0 jit_solution(2708242832434163317)
XLA Ops:
  0.6 6.4 %collective-permute-start = (bf16[16,512]{1,0:T(8,128)(2,1)}, bf16[16,512]{1,0:T(8,128)(2,1)S(1)}, u32[]{:S(2)}, u32[]{:S(2)}) collective-permute-start(bf16[16,512]{1,0:T(8,128)(2,1)} %bitcast.150), channel_id=1, source_target_pairs={{0,128},{128,0},{1,129},{129,1},{2,130},{130,2},{3,131},{131,3},{4... | collective-permute-start | bytes 49160 | tf_op jit(solution)/shard_map/ppermute | solution.py:188
  8.9 1.6 collective-permute-start.1
  10.5 2.3 %collective-permute-start.2 = (bf16[2,16,512]{2,1,0:T(8,128)(2,1)S(1)}, bf16[2,16,512]{2,1,0:T(8,128)(2,1)S(1)}, u32[]{:S(2)}, u32[]{:S(2)}) collective-permute-start(bf16[2,16,512]{2,1,0:T(8,128)(2,1)S(1)} %bitcast_dynamic-update-slice_fusion.20), channel_id=1, source_target_pairs={{0,16},{8,24},{16,0},{24,8},{1,17},{9,25},{17,1},{25,9},{2,18},{10... | collective-permute-start | bytes 98312 | tf_op jit(solution)/shard_map/ppermute | solution.py:188
  15.3 1.4 collective-permute-done.3
  17.8 2.7 %collective-permute-start.5 = (bf16[4,2,16,256]{3,2,1,0:T(8,128)(2,1)S(1)}, bf16[4,2,16,256]{3,2,1,0:T(8,128)(2,1)S(1)}, u32[]{:S(2)}, u32[]{:S(2)}) collective-permute-start(bf16[4,2,16,256]{3,2,1,0:T(8,128)(2,1)S(1)} %get-tuple-element.27), channel_id=1, source_target_pairs={{0,64},{32,96},{64,0},{96,32},{1,65},{33,97},{65,1},{97,33},{2,66}... | collective-permute-start | bytes 196616 | tf_op jit(solution)/shard_map/ppermute | solution.py:188
  20.5 1.4 collective-permute-start.6
  22.0 1.6 collective-permute-start.10
  23.6 2.9 %collective-permute-start.11 = (bf16[4,2,16,256]{3,2,1,0:T(8,128)(2,1)S(1)}, bf16[4,2,16,256]{3,2,1,0:T(8,128)(2,1)S(1)}, u32[]{:S(2)}, u32[]{:S(2)}) collective-permute-start(bf16[4,2,16,256]{3,2,1,0:T(8,128)(2,1)S(1)} %get-tuple-element.28), channel_id=1, source_target_pairs={{0,4},{2,6},{4,0},{6,2},{1,5},{3,7},{5,1},{7,3},{8,12},{10,14},{12... | collective-permute-start | bytes 196616 | tf_op jit(solution)/shard_map/ppermute | solution.py:188
  26.6 1.4 collective-permute-start.12
  29.6 2.0 %collective-permute-start.9 = (bf16[4,4,2,16,256]{4,3,2,1,0:T(8,128)(2,1)S(1)}, bf16[4,4,2,16,256]{4,3,2,1,0:T(8,128)(2,1)S(1)}, u32[]{:S(2)}, u32[]{:S(2)}) collective-permute-start(bf16[4,4,2,16,256]{4,3,2,1,0:T(8,128)(2,1)S(1)} %bitcast_dynamic-update-slice_fusion.12), channel_id=1, source_target_pairs={{0,6},{2,0},{4,2},{6,4},{1,7},{3,1},{5,3},{7,5},{8,14},{10,8},{12,... | collective-permute-start | bytes 786440 | tf_op jit(solution)/shard_map/ppermute | solution.py:188
  32.4 2.6 %collective-permute-start.14 = (bf16[4,4,2,16,256]{4,3,2,1,0:T(8,128)(2,1)S(1)}, bf16[4,4,2,16,256]{4,3,2,1,0:T(8,128)(2,1)S(1)}, u32[]{:S(2)}, u32[]{:S(2)}) collective-permute-start(bf16[4,4,2,16,256]{4,3,2,1,0:T(8,128)(2,1)S(1)} %bitcast_dynamic-update-slice_fusion.8), channel_id=1, source_target_pairs={{0,64},{32,96},{64,0},{96,32},{1,65},{33,97},{65,1},{97,33},{2,66}... | collective-permute-start | bytes 786440 | tf_op jit(solution)/shard_map/ppermute | solution.py:188
  35.3 4.3 %collective-permute-done.7 = bf16[4,4,2,16,256]{4,3,2,1,0:T(8,128)(2,1)S(1)} collective-permute-done((bf16[4,4,2,16,256]{4,3,2,1,0:T(8,128)(2,1)S(1)}, bf16[4,4,2,16,256]{4,3,2,1,0:T(8,128)(2,1)S(1)}, u32[]{:S(2)}, u32[]{:S(2)}) %collective-permute-start.7) | collective-permute-done | bytes 262176 | tf_op jit(solution)/shard_map/ppermute | solution.py:188
  40.4 1.7 %collective-permute-done.14 = bf16[4,4,2,16,256]{4,3,2,1,0:T(8,128)(2,1)S(1)} collective-permute-done((bf16[4,4,2,16,256]{4,3,2,1,0:T(8,128)(2,1)S(1)}, bf16[4,4,2,16,256]{4,3,2,1,0:T(8,128)(2,1)S(1)}, u32[]{:S(2)}, u32[]{:S(2)}) %collective-permute-start.14) | collective-permute-done | bytes 262176 | tf_op jit(solution)/shard_map/ppermute | solution.py:188
  42.2 3.8 %collective-permute-done.15 = bf16[4,4,2,16,256]{4,3,2,1,0:T(8,128)(2,1)S(1)} collective-permute-done((bf16[4,4,2,16,256]{4,3,2,1,0:T(8,128)(2,1)S(1)}, bf16[4,4,2,16,256]{4,3,2,1,0:T(8,128)(2,1)S(1)}, u32[]{:S(2)}, u32[]{:S(2)}) %collective-permute-start.15) | collective-permute-done | bytes 262176 | tf_op jit(solution)/shard_map/ppermute | solution.py:188
  46.9 4.0 %collective-permute-done.16.v_ref = bf16[4,4,128,512]{3,2,1,0:T(8,128)(2,1)} collective-permute-done((bf16[4,4,128,512]{3,2,1,0:T(8,128)(2,1)S(1)}, bf16[4,4,128,512]{3,2,1,0:T(8,128)(2,1)}, u32[]{:S(2)}, u32[]{:S(2)}) %collective-permute-start.16) | collective-permute-done | bytes 2097184 | tf_op jit(solution)/shard_map/ppermute | solution.py:212
  50.9 19.8 %shard_map.68 = (f32[8,128,512]{2,1,0:T(8,128)}, f32[4,4,128,512]{3,2,1,0:T(8,128)}) custom-call(s32[192]{0:T(256)S(1)} %reshape_squeeze.3.rows_ref, s32[32]{0:T(128)S(1)} %bitcast.146, s32[1]{0:T(128)} %bitcast.36.sel_ref, bf16[8,128,512]{2,1,0:T(8,128)(2,1)S(1)} %bitcast.144, bf16[4,4,128,512]{3,2,1,0:T(8,128)(2,1)} %collective-permute-done.16.v_ref, ...), custom_call_target="tpu_custom_call" | custom-call | flops 4831838208 | bytes 14680064 | tf_op jit(solution)/shard_map/pallas_call | solution.py:100
  70.8 21.0 %shard_map.69 = (f32[8,128,512]{2,1,0:T(8,128)}, f32[4,4,128,512]{3,2,1,0:T(8,128)}) custom-call(s32[192]{0:T(256)S(1)} %reshape_squeeze.3.rows_ref, s32[32]{0:T(128)S(1)} %bitcast.147, s32[1]{0:T(128)} %bitcast.1.sel_ref, bf16[8,128,512]{2,1,0:T(8,128)(2,1)S(1)} %bitcast.145, ...), custom_call_target="tpu_custom_call", output_to_operand_aliasing={{0}: (7, {})} | custom-call | flops 4831838208 | bytes 14680064 | tf_op jit(solution)/shard_map/pallas_call | solution.py:100
  91.7 4.5 %slice_add_fusion = (f32[4,4,2,4,16,256]{5,4,3,2,1,0:T(8,128)S(1)}, f32[4,4,2,4,16,256]{5,4,3,2,1,0:T(8,128)S(1)}) fusion(f32[4,4,2,4,16,512]{5,4,3,2,1,0:T(8,128)} %bitcast.39, f32[4,4,2,4,16,512]{5,4,3,2,1,0:T(8,128)} %bitcast.148), kind=kLoop, calls=%fused_computation | loop fusion | flops 1048576 | bytes 12582912 | tf_op jit(solution)/shard_map/add | solution.py:227
  99.1 2.1 %collective-permute-start.25 = (f32[4,4,2,16,256]{4,3,2,1,0:T(8,128)S(1)}, f32[4,4,2,16,256]{4,3,2,1,0:T(8,128)}, u32[]{:S(2)}, u32[]{:S(2)}) collective-permute-start(f32[4,4,2,16,256]{4,3,2,1,0:T(8,128)S(1)} %get-tuple-element.14), channel_id=1, source_target_pairs={{0,64},{32,96},{64,0},{96,32},{1,65},{33,97},{65,1},{97,33},{2,66}... | collective-permute-start | bytes 1572872 | tf_op jit(solution)/shard_map/ppermute | solution.py:177
  103.3 2.8 %collective-permute-start.19 = (f32[4,2,4,16,256]{4,3,2,1,0:T(8,128)}, f32[4,2,4,16,256]{4,3,2,1,0:T(8,128)}, u32[]{:S(2)}, u32[]{:S(2)}) collective-permute-start(f32[4,2,4,16,256]{4,3,2,1,0:T(8,128)} %get-tuple-element.17), channel_id=1, source_target_pairs={{0,4},{2,6},{4,0},{6,2},{1,5},{3,7},{5,1},{7,3},{8,12},{10,14},{12... | collective-permute-start | bytes 1572872 | tf_op jit(solution)/shard_map/ppermute | solution.py:177
  106.1 19.4 %collective-permute-done.24 = f32[4,4,2,16,256]{4,3,2,1,0:T(8,128)} collective-permute-done((f32[4,4,2,16,256]{4,3,2,1,0:T(8,128)}, f32[4,4,2,16,256]{4,3,2,1,0:T(8,128)}, u32[]{:S(2)}, u32[]{:S(2)}) %collective-permute-start.24) | collective-permute-done | bytes 524320 | tf_op jit(solution)/shard_map/ppermute | solution.py:177
  125.9 1.7 %fusion.1 = f32[4,4,2,16,256]{4,3,2,1,0:T(8,128)S(1)} fusion(f32[4,4,2,16,256]{4,3,2,1,0:T(8,128)} %collective-permute-done.26, f32[4,4,2,16,256]{4,3,2,1,0:T(8,128)} %collective-permute-done.25, f32[4,4,2,16,256]{4,3,2,1,0:T(8,128)} %collective-permute-done.24, f32[4,4,2,4,16,256]{5,4,3,2,1,0:T(8,128)} %copy-done.2, s32[]{:T(128)S(6)} %select_n.218), kind=kLoop, calls=%fused_computation.5 | loop fusion | flops 393216 | bytes 2621444 | tf_op jit(solution)/shard_map/add | solution.py:177
  127.7 1.7 %collective-permute-start.27 = (f32[4,2,16,256]{3,2,1,0:T(8,128)S(1)}, f32[4,2,16,256]{3,2,1,0:T(8,128)S(1)}, u32[]{:S(2)}, u32[]{:S(2)}) collective-permute-start(f32[4,2,16,256]{3,2,1,0:T(8,128)S(1)} %get-tuple-element.18), channel_id=1, source_target_pairs={{0,2},{2,4},{4,6},{6,0},{1,3},{3,5},{5,7},{7,1},{8,10},{10,12},{12... | collective-permute-start | bytes 393224 | tf_op jit(solution)/shard_map/ppermute | solution.py:177
  130.4 1.7 %collective-permute-start.29 = (f32[4,2,16,256]{3,2,1,0:T(8,128)S(1)}, f32[4,2,16,256]{3,2,1,0:T(8,128)S(1)}, u32[]{:S(2)}, u32[]{:S(2)}) collective-permute-start(f32[4,2,16,256]{3,2,1,0:T(8,128)S(1)} %get-tuple-element.19), channel_id=1, source_target_pairs={{0,6},{2,0},{4,2},{6,4},{1,7},{3,1},{5,3},{7,5},{8,14},{10,8},{12,... | collective-permute-start | bytes 393224 | tf_op jit(solution)/shard_map/ppermute | solution.py:177
  132.2 5.6 %collective-permute-done.20 = f32[4,2,4,16,256]{4,3,2,1,0:T(8,128)} collective-permute-done((f32[4,2,4,16,256]{4,3,2,1,0:T(8,128)}, f32[4,2,4,16,256]{4,3,2,1,0:T(8,128)}, u32[]{:S(2)}, u32[]{:S(2)}) %collective-permute-start.20) | collective-permute-done | bytes 524320 | tf_op jit(solution)/shard_map/ppermute | solution.py:177
  137.8 1.6 fusion.3
  139.6 3.1 %collective-permute-start.23 = (f32[4,2,16,256]{3,2,1,0:T(8,128)S(1)}, f32[4,2,16,256]{3,2,1,0:T(8,128)S(1)}, u32[]{:S(2)}, u32[]{:S(2)}) collective-permute-start(f32[4,2,16,256]{3,2,1,0:T(8,128)S(1)} %get-tuple-element.22), channel_id=1, source_target_pairs={{0,96},{32,0},{64,32},{96,64},{1,97},{33,1},{65,33},{97,65},{2,98}... | collective-permute-start | bytes 393224 | tf_op jit(solution)/shard_map/ppermute | solution.py:177
  142.8 4.3 %collective-permute-done.21 = f32[4,2,16,256]{3,2,1,0:T(8,128)S(1)} collective-permute-done((f32[4,2,16,256]{3,2,1,0:T(8,128)S(1)}, f32[4,2,16,256]{3,2,1,0:T(8,128)S(1)}, u32[]{:S(2)}, u32[]{:S(2)}) %collective-permute-start.21) | collective-permute-done | bytes 131104 | tf_op jit(solution)/shard_map/ppermute | solution.py:177
  149.3 2.8 %collective-permute-start.31 = (f32[2,16,512]{2,1,0:T(8,128)S(1)}, f32[2,16,512]{2,1,0:T(8,128)S(1)}, u32[]{:S(2)}, u32[]{:S(2)}) collective-permute-start(f32[2,16,512]{2,1,0:T(8,128)S(1)} %get-tuple-element.25), channel_id=1, source_target_pairs={{0,16},{8,24},{16,0},{24,8},{1,17},{9,25},{17,1},{25,9},{2,18},{10... | collective-permute-start | bytes 196616 | tf_op jit(solution)/shard_map/ppermute | solution.py:177
  152.9 2.5 %collective-permute-done.31 = f32[2,16,512]{2,1,0:T(8,128)S(1)} collective-permute-done((f32[2,16,512]{2,1,0:T(8,128)S(1)}, f32[2,16,512]{2,1,0:T(8,128)S(1)}, u32[]{:S(2)}, u32[]{:S(2)}) %collective-permute-start.31) | collective-permute-done | bytes 65568 | tf_op jit(solution)/shard_map/ppermute | solution.py:177
  156.4 5.0 %collective-permute-start.33 = (f32[16,512]{1,0:T(8,128)S(1)}, f32[16,512]{1,0:T(8,128)S(1)}, u32[]{:S(2)}, u32[]{:S(2)}) collective-permute-start(f32[16,512]{1,0:T(8,128)S(1)} %dynamic-slice_bitcast_fusion.12), channel_id=1, source_target_pairs={{0,128},{128,0},{1,129},{129,1},{2,130},{130,2},{3,131},{131,3},{4... | collective-permute-start | bytes 98312 | tf_op jit(solution)/shard_map/ppermute | solution.py:177
  161.4 2.9 %collective-permute-done.33 = f32[16,512]{1,0:T(8,128)S(1)} collective-permute-done((f32[16,512]{1,0:T(8,128)S(1)}, f32[16,512]{1,0:T(8,128)S(1)}, u32[]{:S(2)}, u32[]{:S(2)}) %collective-permute-start.33) | collective-permute-done | bytes 32800 | tf_op jit(solution)/shard_map/ppermute | solution.py:177
  (93 shorter events, 21.4 us)
Async XLA Ops:
  0.6 8.3 %collective-permute-start = (bf16[16,512]{1,0:T(8,128)(2,1)}, bf16[16,512]{1,0:T(8,128)(2,1)S(1)}, u32[]{:S(2)}, u32[]{:S(2)}) collective-permute-start(bf16[16,512]{1,0:T(8,128)(2,1)} %bitcast.150), channel_id=1, source_target_pairs={{0,128},{128,0},{1,129},{129,1},{2,130},{130,2},{3,131},{131,3},{4... | collective-permute-start | bytes 49160 | tf_op jit(solution)/shard_map/ppermute | solution.py:188
  8.9 5.0 %collective-permute-start.1 = (bf16[2,16,512]{2,1,0:T(8,128)(2,1)S(1)}, bf16[2,16,512]{2,1,0:T(8,128)(2,1)S(1)}, u32[]{:S(2)}, u32[]{:S(2)}) collective-permute-start(bf16[2,16,512]{2,1,0:T(8,128)(2,1)S(1)} %bitcast_dynamic-update-slice_fusion.20), channel_id=1, source_target_pairs={{0,8},{8,16},{16,24},{24,0},{1,9},{9,17},{17,25},{25,1},{2,10},{10... | collective-permute-start | bytes 98312 | tf_op jit(solution)/shard_map/ppermute | solution.py:188
  10.5 4.8 %collective-permute-start.2 = (bf16[2,16,512]{2,1,0:T(8,128)(2,1)S(1)}, bf16[2,16,512]{2,1,0:T(8,128)(2,1)S(1)}, u32[]{:S(2)}, u32[]{:S(2)}) collective-permute-start(bf16[2,16,512]{2,1,0:T(8,128)(2,1)S(1)} %bitcast_dynamic-update-slice_fusion.20), channel_id=1, source_target_pairs={{0,16},{8,24},{16,0},{24,8},{1,17},{9,25},{17,1},{25,9},{2,18},{10... | collective-permute-start | bytes 98312 | tf_op jit(solution)/shard_map/ppermute | solution.py:188
  16.7 9.8 %collective-permute-start.4 = (bf16[4,2,16,256]{3,2,1,0:T(8,128)(2,1)S(1)}, bf16[4,2,16,256]{3,2,1,0:T(8,128)(2,1)S(1)}, u32[]{:S(2)}, u32[]{:S(2)}) collective-permute-start(bf16[4,2,16,256]{3,2,1,0:T(8,128)(2,1)S(1)} %get-tuple-element.27), channel_id=1, source_target_pairs={{0,32},{32,64},{64,96},{96,0},{1,33},{33,65},{65,97},{97,1},{2,34}... | collective-permute-start | bytes 196616 | tf_op jit(solution)/shard_map/ppermute | solution.py:188
  17.8 10.2 %collective-permute-start.5 = (bf16[4,2,16,256]{3,2,1,0:T(8,128)(2,1)S(1)}, bf16[4,2,16,256]{3,2,1,0:T(8,128)(2,1)S(1)}, u32[]{:S(2)}, u32[]{:S(2)}) collective-permute-start(bf16[4,2,16,256]{3,2,1,0:T(8,128)(2,1)S(1)} %get-tuple-element.27), channel_id=1, source_target_pairs={{0,64},{32,96},{64,0},{96,32},{1,65},{33,97},{65,1},{97,33},{2,66}... | collective-permute-start | bytes 196616 | tf_op jit(solution)/shard_map/ppermute | solution.py:188
  20.5 7.5 %collective-permute-start.6 = (bf16[4,2,16,256]{3,2,1,0:T(8,128)(2,1)S(1)}, bf16[4,2,16,256]{3,2,1,0:T(8,128)(2,1)S(1)}, u32[]{:S(2)}, u32[]{:S(2)}) collective-permute-start(bf16[4,2,16,256]{3,2,1,0:T(8,128)(2,1)S(1)} %get-tuple-element.27), channel_id=1, source_target_pairs={{0,96},{32,0},{64,32},{96,64},{1,97},{33,1},{65,33},{97,65},{2,98}... | collective-permute-start | bytes 196616 | tf_op jit(solution)/shard_map/ppermute | solution.py:188
  22.0 7.6 %collective-permute-start.10 = (bf16[4,2,16,256]{3,2,1,0:T(8,128)(2,1)S(1)}, bf16[4,2,16,256]{3,2,1,0:T(8,128)(2,1)S(1)}, u32[]{:S(2)}, u32[]{:S(2)}) collective-permute-start(bf16[4,2,16,256]{3,2,1,0:T(8,128)(2,1)S(1)} %get-tuple-element.28), channel_id=1, source_target_pairs={{0,2},{2,4},{4,6},{6,0},{1,3},{3,5},{5,7},{7,1},{8,10},{10,12},{12... | collective-permute-start | bytes 196616 | tf_op jit(solution)/shard_map/ppermute | solution.py:188
  23.6 8.0 %collective-permute-start.11 = (bf16[4,2,16,256]{3,2,1,0:T(8,128)(2,1)S(1)}, bf16[4,2,16,256]{3,2,1,0:T(8,128)(2,1)S(1)}, u32[]{:S(2)}, u32[]{:S(2)}) collective-permute-start(bf16[4,2,16,256]{3,2,1,0:T(8,128)(2,1)S(1)} %get-tuple-element.28), channel_id=1, source_target_pairs={{0,4},{2,6},{4,0},{6,2},{1,5},{3,7},{5,1},{7,3},{8,12},{10,14},{12... | collective-permute-start | bytes 196616 | tf_op jit(solution)/shard_map/ppermute | solution.py:188
  26.6 5.1 %collective-permute-start.12 = (bf16[4,2,16,256]{3,2,1,0:T(8,128)(2,1)S(1)}, bf16[4,2,16,256]{3,2,1,0:T(8,128)(2,1)S(1)}, u32[]{:S(2)}, u32[]{:S(2)}) collective-permute-start(bf16[4,2,16,256]{3,2,1,0:T(8,128)(2,1)S(1)} %get-tuple-element.28), channel_id=1, source_target_pairs={{0,6},{2,0},{4,2},{6,4},{1,7},{3,1},{5,3},{7,5},{8,14},{10,8},{12,... | collective-permute-start | bytes 196616 | tf_op jit(solution)/shard_map/ppermute | solution.py:188
  28.1 11.5 %collective-permute-start.7 = (bf16[4,4,2,16,256]{4,3,2,1,0:T(8,128)(2,1)S(1)}, bf16[4,4,2,16,256]{4,3,2,1,0:T(8,128)(2,1)S(1)}, u32[]{:S(2)}, u32[]{:S(2)}) collective-permute-start(bf16[4,4,2,16,256]{4,3,2,1,0:T(8,128)(2,1)S(1)} %bitcast_dynamic-update-slice_fusion.12), channel_id=1, source_target_pairs={{0,2},{2,4},{4,6},{6,0},{1,3},{3,5},{5,7},{7,1},{8,10},{10,12},{12... | collective-permute-start | bytes 786440 | tf_op jit(solution)/shard_map/ppermute | solution.py:188
  28.8 10.8 %collective-permute-start.8 = (bf16[4,4,2,16,256]{4,3,2,1,0:T(8,128)(2,1)S(1)}, bf16[4,4,2,16,256]{4,3,2,1,0:T(8,128)(2,1)S(1)}, u32[]{:S(2)}, u32[]{:S(2)}) collective-permute-start(bf16[4,4,2,16,256]{4,3,2,1,0:T(8,128)(2,1)S(1)} %bitcast_dynamic-update-slice_fusion.12), channel_id=1, source_target_pairs={{0,4},{2,6},{4,0},{6,2},{1,5},{3,7},{5,1},{7,3},{8,12},{10,14},{12... | collective-permute-start | bytes 786440 | tf_op jit(solution)/shard_map/ppermute | solution.py:188
  29.6 10.7 %collective-permute-start.9 = (bf16[4,4,2,16,256]{4,3,2,1,0:T(8,128)(2,1)S(1)}, bf16[4,4,2,16,256]{4,3,2,1,0:T(8,128)(2,1)S(1)}, u32[]{:S(2)}, u32[]{:S(2)}) collective-permute-start(bf16[4,4,2,16,256]{4,3,2,1,0:T(8,128)(2,1)S(1)} %bitcast_dynamic-update-slice_fusion.12), channel_id=1, source_target_pairs={{0,6},{2,0},{4,2},{6,4},{1,7},{3,1},{5,3},{7,5},{8,14},{10,8},{12,... | collective-permute-start | bytes 786440 | tf_op jit(solution)/shard_map/ppermute | solution.py:188
  31.7 8.7 %collective-permute-start.13 = (bf16[4,4,2,16,256]{4,3,2,1,0:T(8,128)(2,1)S(1)}, bf16[4,4,2,16,256]{4,3,2,1,0:T(8,128)(2,1)S(1)}, u32[]{:S(2)}, u32[]{:S(2)}) collective-permute-start(bf16[4,4,2,16,256]{4,3,2,1,0:T(8,128)(2,1)S(1)} %bitcast_dynamic-update-slice_fusion.8), channel_id=1, source_target_pairs={{0,32},{32,64},{64,96},{96,0},{1,33},{33,65},{65,97},{97,1},{2,34}... | collective-permute-start | bytes 786440 | tf_op jit(solution)/shard_map/ppermute | solution.py:188
  32.4 9.8 %collective-permute-start.14 = (bf16[4,4,2,16,256]{4,3,2,1,0:T(8,128)(2,1)S(1)}, bf16[4,4,2,16,256]{4,3,2,1,0:T(8,128)(2,1)S(1)}, u32[]{:S(2)}, u32[]{:S(2)}) collective-permute-start(bf16[4,4,2,16,256]{4,3,2,1,0:T(8,128)(2,1)S(1)} %bitcast_dynamic-update-slice_fusion.8), channel_id=1, source_target_pairs={{0,64},{32,96},{64,0},{96,32},{1,65},{33,97},{65,1},{97,33},{2,66}... | collective-permute-start | bytes 786440 | tf_op jit(solution)/shard_map/ppermute | solution.py:188
  39.6 6.4 %collective-permute-start.15 = (bf16[4,4,2,16,256]{4,3,2,1,0:T(8,128)(2,1)S(1)}, bf16[4,4,2,16,256]{4,3,2,1,0:T(8,128)(2,1)S(1)}, u32[]{:S(2)}, u32[]{:S(2)}) collective-permute-start(bf16[4,4,2,16,256]{4,3,2,1,0:T(8,128)(2,1)S(1)} %bitcast_dynamic-update-slice_fusion.8), channel_id=1, source_target_pairs={{0,96},{32,0},{64,32},{96,64},{1,97},{33,1},{65,33},{97,65},{2,98}... | collective-permute-start | bytes 786440 | tf_op jit(solution)/shard_map/ppermute | solution.py:188
  46.3 4.6 %collective-permute-start.16 = (bf16[4,4,128,512]{3,2,1,0:T(8,128)(2,1)S(1)}, bf16[4,4,128,512]{3,2,1,0:T(8,128)(2,1)}, u32[]{:S(2)}, u32[]{:S(2)}) collective-permute-start(bf16[4,4,128,512]{3,2,1,0:T(8,128)(2,1)S(1)} %bitcast.142), channel_id=1, source_target_pairs={{0,1},{1,0},{2,3},{3,2},{4,5},{5,4},{6,7},{7,6},{8,9},{9,8},{10,11... | collective-permute-start | bytes 6291464 | tf_op jit(solution)/shard_map/ppermute | solution.py:212
  70.6 21.1 %collective-permute-start.17 = (f32[4,4,128,512]{3,2,1,0:T(8,128)}, f32[4,4,128,512]{3,2,1,0:T(8,128)}, u32[]{:S(2)}, u32[]{:S(2)}) collective-permute-start(f32[4,4,128,512]{3,2,1,0:T(8,128)} %get-tuple-element.9), channel_id=1, source_target_pairs={{0,1},{1,0},{2,3},{3,2},{4,5},{5,4},{6,7},{7,6},{8,9},{9,8},{10,11... | collective-permute-start | bytes 12582920 | tf_op jit(solution)/shard_map/ppermute | solution.py:219
  98.5 27.0 %collective-permute-start.24 = (f32[4,4,2,16,256]{4,3,2,1,0:T(8,128)}, f32[4,4,2,16,256]{4,3,2,1,0:T(8,128)}, u32[]{:S(2)}, u32[]{:S(2)}) collective-permute-start(f32[4,4,2,16,256]{4,3,2,1,0:T(8,128)} %get-tuple-element.12), channel_id=1, source_target_pairs={{0,32},{32,64},{64,96},{96,0},{1,33},{33,65},{65,97},{97,1},{2,34}... | collective-permute-start | bytes 1572872 | tf_op jit(solution)/shard_map/ppermute | solution.py:177
  99.1 26.3 %collective-permute-start.25 = (f32[4,4,2,16,256]{4,3,2,1,0:T(8,128)S(1)}, f32[4,4,2,16,256]{4,3,2,1,0:T(8,128)}, u32[]{:S(2)}, u32[]{:S(2)}) collective-permute-start(f32[4,4,2,16,256]{4,3,2,1,0:T(8,128)S(1)} %get-tuple-element.14), channel_id=1, source_target_pairs={{0,64},{32,96},{64,0},{96,32},{1,65},{33,97},{65,1},{97,33},{2,66}... | collective-permute-start | bytes 1572872 | tf_op jit(solution)/shard_map/ppermute | solution.py:177
  101.2 24.7 %collective-permute-start.26 = (f32[4,4,2,16,256]{4,3,2,1,0:T(8,128)S(1)}, f32[4,4,2,16,256]{4,3,2,1,0:T(8,128)}, u32[]{:S(2)}, u32[]{:S(2)}) collective-permute-start(f32[4,4,2,16,256]{4,3,2,1,0:T(8,128)S(1)} %get-tuple-element.13), channel_id=1, source_target_pairs={{0,96},{32,0},{64,32},{96,64},{1,97},{33,1},{65,33},{97,65},{2,98}... | collective-permute-start | bytes 1572872 | tf_op jit(solution)/shard_map/ppermute | solution.py:177
  103.3 27.1 %collective-permute-start.18 = (f32[4,2,4,16,256]{4,3,2,1,0:T(8,128)}, f32[4,2,4,16,256]{4,3,2,1,0:T(8,128)}, u32[]{:S(2)}, u32[]{:S(2)}) collective-permute-start(f32[4,2,4,16,256]{4,3,2,1,0:T(8,128)} %get-tuple-element.15), channel_id=1, source_target_pairs={{0,2},{2,4},{4,6},{6,0},{1,3},{3,5},{5,7},{7,1},{8,10},{10,12},{12... | collective-permute-start | bytes 1572872 | tf_op jit(solution)/shard_map/ppermute | solution.py:177
  103.3 28.9 %collective-permute-start.19 = (f32[4,2,4,16,256]{4,3,2,1,0:T(8,128)}, f32[4,2,4,16,256]{4,3,2,1,0:T(8,128)}, u32[]{:S(2)}, u32[]{:S(2)}) collective-permute-start(f32[4,2,4,16,256]{4,3,2,1,0:T(8,128)} %get-tuple-element.17), channel_id=1, source_target_pairs={{0,4},{2,6},{4,0},{6,2},{1,5},{3,7},{5,1},{7,3},{8,12},{10,14},{12... | collective-permute-start | bytes 1572872 | tf_op jit(solution)/shard_map/ppermute | solution.py:177
  125.5 12.3 %collective-permute-start.20 = (f32[4,2,4,16,256]{4,3,2,1,0:T(8,128)}, f32[4,2,4,16,256]{4,3,2,1,0:T(8,128)}, u32[]{:S(2)}, u32[]{:S(2)}) collective-permute-start(f32[4,2,4,16,256]{4,3,2,1,0:T(8,128)} %get-tuple-element.16), channel_id=1, source_target_pairs={{0,6},{2,0},{4,2},{6,4},{1,7},{3,1},{5,3},{7,5},{8,14},{10,8},{12,... | collective-permute-start | bytes 1572872 | tf_op jit(solution)/shard_map/ppermute | solution.py:177
  127.7 11.9 %collective-permute-start.27 = (f32[4,2,16,256]{3,2,1,0:T(8,128)S(1)}, f32[4,2,16,256]{3,2,1,0:T(8,128)S(1)}, u32[]{:S(2)}, u32[]{:S(2)}) collective-permute-start(f32[4,2,16,256]{3,2,1,0:T(8,128)S(1)} %get-tuple-element.18), channel_id=1, source_target_pairs={{0,2},{2,4},{4,6},{6,0},{1,3},{3,5},{5,7},{7,1},{8,10},{10,12},{12... | collective-permute-start | bytes 393224 | tf_op jit(solution)/shard_map/ppermute | solution.py:177
  129.4 13.4 %collective-permute-start.28 = (f32[4,2,16,256]{3,2,1,0:T(8,128)S(1)}, f32[4,2,16,256]{3,2,1,0:T(8,128)S(1)}, u32[]{:S(2)}, u32[]{:S(2)}) collective-permute-start(f32[4,2,16,256]{3,2,1,0:T(8,128)S(1)} %get-tuple-element.20), channel_id=1, source_target_pairs={{0,4},{2,6},{4,0},{6,2},{1,5},{3,7},{5,1},{7,3},{8,12},{10,14},{12... | collective-permute-start | bytes 393224 | tf_op jit(solution)/shard_map/ppermute | solution.py:177
  130.4 12.3 %collective-permute-start.29 = (f32[4,2,16,256]{3,2,1,0:T(8,128)S(1)}, f32[4,2,16,256]{3,2,1,0:T(8,128)S(1)}, u32[]{:S(2)}, u32[]{:S(2)}) collective-permute-start(f32[4,2,16,256]{3,2,1,0:T(8,128)S(1)} %get-tuple-element.19), channel_id=1, source_target_pairs={{0,6},{2,0},{4,2},{6,4},{1,7},{3,1},{5,3},{7,5},{8,14},{10,8},{12,... | collective-permute-start | bytes 393224 | tf_op jit(solution)/shard_map/ppermute | solution.py:177
  139.4 7.7 %collective-permute-start.21 = (f32[4,2,16,256]{3,2,1,0:T(8,128)S(1)}, f32[4,2,16,256]{3,2,1,0:T(8,128)S(1)}, u32[]{:S(2)}, u32[]{:S(2)}) collective-permute-start(f32[4,2,16,256]{3,2,1,0:T(8,128)S(1)} %get-tuple-element.21), channel_id=1, source_target_pairs={{0,32},{32,64},{64,96},{96,0},{1,33},{33,65},{65,97},{97,1},{2,34}... | collective-permute-start | bytes 393224 | tf_op jit(solution)/shard_map/ppermute | solution.py:177
  139.5 7.6 %collective-permute-start.22 = (f32[4,2,16,256]{3,2,1,0:T(8,128)S(1)}, f32[4,2,16,256]{3,2,1,0:T(8,128)S(1)}, u32[]{:S(2)}, u32[]{:S(2)}) collective-permute-start(f32[4,2,16,256]{3,2,1,0:T(8,128)S(1)} %get-tuple-element.23), channel_id=1, source_target_pairs={{0,64},{32,96},{64,0},{96,32},{1,65},{33,97},{65,1},{97,33},{2,66}... | collective-permute-start | bytes 393224 | tf_op jit(solution)/shard_map/ppermute | solution.py:177
  139.6 8.4 %collective-permute-start.23 = (f32[4,2,16,256]{3,2,1,0:T(8,128)S(1)}, f32[4,2,16,256]{3,2,1,0:T(8,128)S(1)}, u32[]{:S(2)}, u32[]{:S(2)}) collective-permute-start(f32[4,2,16,256]{3,2,1,0:T(8,128)S(1)} %get-tuple-element.22), channel_id=1, source_target_pairs={{0,96},{32,0},{64,32},{96,64},{1,97},{33,1},{65,33},{97,65},{2,98}... | collective-permute-start | bytes 393224 | tf_op jit(solution)/shard_map/ppermute | solution.py:177
  148.1 4.8 %collective-permute-start.30 = (f32[2,16,512]{2,1,0:T(8,128)S(1)}, f32[2,16,512]{2,1,0:T(8,128)S(1)}, u32[]{:S(2)}, u32[]{:S(2)}) collective-permute-start(f32[2,16,512]{2,1,0:T(8,128)S(1)} %get-tuple-element.24), channel_id=1, source_target_pairs={{0,8},{8,16},{16,24},{24,0},{1,9},{9,17},{17,25},{25,1},{2,10},{10... | collective-permute-start | bytes 196616 | tf_op jit(solution)/shard_map/ppermute | solution.py:177
  149.3 6.1 %collective-permute-start.31 = (f32[2,16,512]{2,1,0:T(8,128)S(1)}, f32[2,16,512]{2,1,0:T(8,128)S(1)}, u32[]{:S(2)}, u32[]{:S(2)}) collective-permute-start(f32[2,16,512]{2,1,0:T(8,128)S(1)} %get-tuple-element.25), channel_id=1, source_target_pairs={{0,16},{8,24},{16,0},{24,8},{1,17},{9,25},{17,1},{25,9},{2,18},{10... | collective-permute-start | bytes 196616 | tf_op jit(solution)/shard_map/ppermute | solution.py:177
  156.4 7.9 %collective-permute-start.33 = (f32[16,512]{1,0:T(8,128)S(1)}, f32[16,512]{1,0:T(8,128)S(1)}, u32[]{:S(2)}, u32[]{:S(2)}) collective-permute-start(f32[16,512]{1,0:T(8,128)S(1)} %dynamic-slice_bitcast_fusion.12), channel_id=1, source_target_pairs={{0,128},{128,0},{1,129},{129,1},{2,130},{130,2},{3,131},{131,3},{4... | collective-permute-start | bytes 98312 | tf_op jit(solution)/shard_map/ppermute | solution.py:177
  (7 other events, 45.0 us)
